TPU v7x, 32 devices: a whole 2x2x4 slice. The times are simulated.
32 devices in a mesh: dp: 8 (over y, x, core), tensor: 4 (over z).
Axes of the slice: x: 2, y: 2, z: 4, core: 2. Of those that a mesh axis runs over, the one named last changes fastest.
Arguments:
- inputs: bfloat16 [4096, 2048], P('dp'), may hold values from -6 to 6
- active: int32 [4096], P('dp'), may hold values from 0 to 1, as said below
- block_table: int32 [16], replicated, may hold values from 0 to 15, as said below
- gain_one: bfloat16 [2048], replicated, may hold values from 0.099609375 to 1.8984375
- w_query: bfloat16 [2048, 2048], P(None, 'tensor'), may hold values from -0.125 to 0.125
- w_key: bfloat16 [2048, 1024], P(None, 'tensor'), may hold values from -0.125 to 0.125
- w_value: bfloat16 [2048, 1024], P(None, 'tensor'), may hold values from -0.125 to 0.125
- w_out: bfloat16 [2048, 2048], P('tensor'), may hold values from -4 to 4
- gain_two: bfloat16 [2048], replicated, may hold values from 0.099609375 to 1.8984375
- w_gate: bfloat16 [2048, 5632], P(None, 'tensor'), may hold values from -0.125 to 0.125
- w_up: bfloat16 [2048, 5632], P(None, 'tensor'), may hold values from -0.125 to 0.125
- w_down: bfloat16 [5632, 2048], P('tensor'), may hold values from -0.078125 to 0.078125
- cotangent: bfloat16 [4096, 2048], P('dp'), may hold values from -6 to 6
Outputs:
- output: bfloat16 [4096, 2048], P('dp')
- grad_input: float32 [4096, 2048], P('dp')
- grad_gain_one: float32 [2048], replicated
- grad_w_query: float32 [2048, 2048], P(None, 'tensor')
- grad_w_key: float32 [2048, 1024], P(None, 'tensor')
- grad_w_value: float32 [2048, 1024], P(None, 'tensor')
- grad_w_out: float32 [2048, 2048], P('tensor')
- grad_gain_two: float32 [2048], replicated
- grad_w_gate: float32 [2048, 5632], P(None, 'tensor')
- grad_w_up: float32 [2048, 5632], P(None, 'tensor')
- grad_w_down: float32 [5632, 2048], P('tensor')
Inputs may be any that keep to these rules, and one draw needn't show every extreme that they name: `active`: 0 or 1 for every token; the share of 1s differs from one causal block to another. `block_table`: each causal block appears once; entries 2i and 2i+1 sum to 15.
All inputs are finite; a program needn't handle non-finite values.
Results may differ from a plain program's by a relative error of at most 0.014.
Values may be sent and summed in bfloat16 or wider, within the bound.
No kernel may reach another device: no remote copies, remote signals or barrier semaphores. Data moves between devices by JAX's collectives and lax.ppermute only.
A program may use at most 256 MiB of HBM per device.

v0:
```python
import jax
import jax.numpy as jnp
from jax import lax
from jax.sharding import PartitionSpec as P

HEAD_DIM = 128


EPS = 1e-05
MASKED_SCORE = -1e30


def rms_norm(values, scales):
    return values * lax.rsqrt(jnp.mean(values * values, axis=-1, keepdims=True) + EPS) * scales


def rotate(values, cos_table, sin_table):
    middle = values.shape[-1] // 2
    leading = values[..., :middle]
    trailing = values[..., middle:]
    return jnp.concatenate(
        [leading * cos_table - trailing * sin_table, trailing * cos_table + leading * sin_table],
        axis=-1,
    )


def angles_of(positions, head_size):
    frequency = 10000.0 ** (-jnp.arange(0, head_size, 2, dtype=jnp.float32) / head_size)
    angles = positions.astype(jnp.float32)[:, None] * frequency[None, :]
    return (jnp.cos(angles)[:, None, :], jnp.sin(angles)[:, None, :])


def swiglu(gate_value, up_value):
    return jax.nn.silu(gate_value) * up_value


def left_trans(left, right):
    return lax.dot_general(
        left, right, (((0,), (0,)), ((), ())), preferred_element_type=jnp.float32
    )


def right_trans(left, right):
    return lax.dot_general(
        left, right, (((1,), (1,)), ((), ())), preferred_element_type=jnp.float32
    )


def on_device(
    inputs,
    active,
    block_table,
    gain_one,
    w_query,
    w_key,
    w_value,
    w_out,
    gain_two,
    w_gate,
    w_up,
    w_down,
    cotangent,
):
    row_count = inputs.shape[0]
    local_heads = w_query.shape[1] // HEAD_DIM
    local_groups = w_key.shape[1] // HEAD_DIM
    group_size = local_heads // local_groups
    half_rows = row_count // 2
    length = row_count * lax.axis_size("dp")
    score_scale = HEAD_DIM ** (-0.5)
    key_pos = (
        block_table[:, None] * half_rows + jnp.arange(half_rows, dtype=jnp.int32)[None, :]
    ).reshape(length)
    row_start = lax.axis_index("dp") * row_count
    query_pos = lax.dynamic_slice_in_dim(key_pos, row_start, row_count)
    slot_ids = jnp.arange(length, dtype=jnp.int32)
    own_ids = row_start + jnp.arange(row_count, dtype=jnp.int32)
    cos_table, sin_table = angles_of(query_pos, HEAD_DIM)
    keep_rows = active.astype(jnp.float32)[:, None]
    source = inputs.astype(jnp.float32)
    normed_full, norm_one_back = jax.vjp(rms_norm, source, gain_one.astype(jnp.float32))
    normed = normed_full.astype(jnp.bfloat16)
    query_raw = jnp.dot(normed, w_query, preferred_element_type=jnp.float32).reshape(
        row_count, local_heads, HEAD_DIM
    )
    key_raw = jnp.dot(normed, w_key, preferred_element_type=jnp.float32).reshape(
        row_count, local_groups, HEAD_DIM
    )
    value_low = jnp.dot(normed, w_value, preferred_element_type=jnp.float32).astype(jnp.bfloat16)
    query_low = (
        rotate(query_raw, cos_table, sin_table)
        .reshape(row_count, local_heads * HEAD_DIM)
        .astype(jnp.bfloat16)
    )
    key_low = (
        rotate(key_raw, cos_table, sin_table)
        .reshape(row_count, local_groups * HEAD_DIM)
        .astype(jnp.bfloat16)
    )
    alive_low = active.astype(jnp.bfloat16)

    def allowed_of(alive_all):
        return (key_pos[None, :] <= query_pos[:, None]) & (
            (alive_all[None, :] > 0) | (slot_ids[None, :] == own_ids[:, None])
        )

    def head_scores(head_index, keys_all, allowed):
        query_part = query_low[:, head_index * HEAD_DIM : (head_index + 1) * HEAD_DIM]
        group_index = head_index // group_size
        key_part = keys_all[:, group_index * HEAD_DIM : (group_index + 1) * HEAD_DIM]
        raw_scores = right_trans(query_part, key_part) * score_scale
        return jnp.where(allowed, raw_scores, MASKED_SCORE)

    all_keys, all_values, all_alive = (
        lax.all_gather(key_low, "dp", axis=0, tiled=True),
        lax.all_gather(value_low, "dp", axis=0, tiled=True),
        lax.all_gather(alive_low, "dp", axis=0, tiled=True),
    )
    allowed_fwd = allowed_of(all_alive)
    mixed_parts = []
    lse_parts = []
    for head_index in range(local_heads):
        masked = head_scores(head_index, all_keys, allowed_fwd)
        row_max = jnp.max(masked, axis=1, keepdims=True)
        shifted = jnp.exp(masked - row_max)
        row_total = jnp.sum(shifted, axis=1, keepdims=True)
        probs_low = (shifted / row_total).astype(jnp.bfloat16)
        lse_parts.append(row_max + jnp.log(row_total))
        group_index = head_index // group_size
        value_part = all_values[:, group_index * HEAD_DIM : (group_index + 1) * HEAD_DIM]
        mixed_parts.append(jnp.dot(probs_low, value_part, preferred_element_type=jnp.float32))
    attended = jnp.concatenate(mixed_parts, axis=1).astype(jnp.bfloat16)
    branch = lax.psum(jnp.dot(attended, w_out, preferred_element_type=jnp.float32), "tensor")
    middle = source + keep_rows * branch
    normed_two_full, norm_two_back = jax.vjp(rms_norm, middle, gain_two.astype(jnp.float32))
    normed_two = normed_two_full.astype(jnp.bfloat16)
    gate_value = jnp.dot(normed_two, w_gate, preferred_element_type=jnp.float32)
    up_value = jnp.dot(normed_two, w_up, preferred_element_type=jnp.float32)
    hidden_full, swiglu_back = jax.vjp(swiglu, gate_value, up_value)
    hidden = hidden_full.astype(jnp.bfloat16)
    down_sum = lax.psum(
        jnp.dot(hidden, w_down, preferred_element_type=jnp.float32).astype(jnp.bfloat16), "tensor"
    ).astype(jnp.float32)
    output = (middle + keep_rows * down_sum).astype(jnp.bfloat16)
    grad_out = cotangent.astype(jnp.float32)
    d_down = (keep_rows * grad_out).astype(jnp.bfloat16)
    grad_w_down = left_trans(hidden, d_down)
    d_hidden = right_trans(d_down, w_down)
    d_gate_full, d_up_full = swiglu_back(d_hidden)
    d_gate = d_gate_full.astype(jnp.bfloat16)
    d_up = d_up_full.astype(jnp.bfloat16)
    grad_w_gate = left_trans(normed_two, d_gate)
    grad_w_up = left_trans(normed_two, d_up)
    d_normed_two = lax.psum(right_trans(d_gate, w_gate) + right_trans(d_up, w_up), "tensor")
    d_middle_norm, grad_gain_two = norm_two_back(d_normed_two)
    grad_middle = grad_out + d_middle_norm
    d_branch = (keep_rows * grad_middle).astype(jnp.bfloat16)
    grad_w_out = left_trans(attended, d_branch)
    d_attended = right_trans(d_branch, w_out).astype(jnp.bfloat16)
    back_keys, back_values, back_alive = (
        lax.all_gather(key_low, "dp", axis=0, tiled=True),
        lax.all_gather(value_low, "dp", axis=0, tiled=True),
        lax.all_gather(alive_low, "dp", axis=0, tiled=True),
    )
    allowed_back = allowed_of(back_alive)
    d_query_parts = []
    d_key_parts = [
        jnp.zeros((length, HEAD_DIM), jnp.float32) for group_index in range(local_groups)
    ]
    d_value_parts = [
        jnp.zeros((length, HEAD_DIM), jnp.float32) for group_index in range(local_groups)
    ]
    for head_index in range(local_heads):
        group_index = head_index // group_size
        masked = head_scores(head_index, back_keys, allowed_back)
        probs = jnp.where(allowed_back, jnp.exp(masked - lse_parts[head_index]), 0.0)
        probs_low = probs.astype(jnp.bfloat16)
        d_out_part = d_attended[:, head_index * HEAD_DIM : (head_index + 1) * HEAD_DIM]
        key_part = back_keys[:, group_index * HEAD_DIM : (group_index + 1) * HEAD_DIM]
        value_part = back_values[:, group_index * HEAD_DIM : (group_index + 1) * HEAD_DIM]
        query_part = query_low[:, head_index * HEAD_DIM : (head_index + 1) * HEAD_DIM]
        d_probs = right_trans(d_out_part, value_part)
        row_delta = jnp.sum(probs * d_probs, axis=1, keepdims=True)
        d_scores = (probs * (d_probs - row_delta)).astype(jnp.bfloat16)
        d_query_parts.append(
            jnp.dot(d_scores, key_part, preferred_element_type=jnp.float32) * score_scale
        )
        d_key_parts[group_index] = (
            d_key_parts[group_index] + left_trans(d_scores, query_part) * score_scale
        )
        d_value_parts[group_index] = d_value_parts[group_index] + left_trans(probs_low, d_out_part)
    d_key_all = jnp.concatenate(d_key_parts, axis=1)
    d_value_all = jnp.concatenate(d_value_parts, axis=1)
    d_key_own, d_value_own = (
        lax.psum_scatter(d_key_all, "dp", scatter_dimension=0, tiled=True),
        lax.psum_scatter(d_value_all, "dp", scatter_dimension=0, tiled=True),
    )
    d_queries = jnp.concatenate(d_query_parts, axis=1).reshape(row_count, local_heads, HEAD_DIM)
    d_query_low = (
        rotate(d_queries, cos_table, -sin_table)
        .reshape(row_count, local_heads * HEAD_DIM)
        .astype(jnp.bfloat16)
    )
    d_key_low = (
        rotate(d_key_own.reshape(row_count, local_groups, HEAD_DIM), cos_table, -sin_table)
        .reshape(row_count, local_groups * HEAD_DIM)
        .astype(jnp.bfloat16)
    )
    d_value_low = d_value_own.astype(jnp.bfloat16)
    grad_w_query = left_trans(normed, d_query_low)
    grad_w_key = left_trans(normed, d_key_low)
    grad_w_value = left_trans(normed, d_value_low)
    d_normed_part = (
        right_trans(d_query_low, w_query)
        + right_trans(d_key_low, w_key)
        + right_trans(d_value_low, w_value)
    )
    d_normed = lax.psum(d_normed_part, "tensor")
    d_source_norm, grad_gain_one = norm_one_back(d_normed)
    grad_input = grad_middle + d_source_norm
    (
        grad_gain_one,
        grad_w_query,
        grad_w_key,
        grad_w_value,
        grad_w_out,
        grad_gain_two,
        grad_w_gate,
        grad_w_up,
        grad_w_down,
    ) = lax.psum(
        (
            grad_gain_one,
            grad_w_query,
            grad_w_key,
            grad_w_value,
            grad_w_out,
            grad_gain_two,
            grad_w_gate,
            grad_w_up,
            grad_w_down,
        ),
        "dp",
    )
    return (
        output,
        grad_input,
        grad_gain_one,
        grad_w_query,
        grad_w_key,
        grad_w_value,
        grad_w_out,
        grad_gain_two,
        grad_w_gate,
        grad_w_up,
        grad_w_down,
    )


def solution(mesh):
    placed = (
        P("dp", None),
        P("dp"),
        P(),
        P(),
        P(None, "tensor"),
        P(None, "tensor"),
        P(None, "tensor"),
        P("tensor", None),
        P(),
        P(None, "tensor"),
        P(None, "tensor"),
        P("tensor", None),
        P("dp", None),
    )
    return jax.shard_map(
        on_device,
        mesh=mesh,
        in_specs=placed,
        out_specs=(
            P("dp", None),
            P("dp", None),
            P(),
            P(None, "tensor"),
            P(None, "tensor"),
            P(None, "tensor"),
            P("tensor", None),
            P(),
            P(None, "tensor"),
            P(None, "tensor"),
            P("tensor", None),
        ),
        check_vma=False,
    )
```

profile of v0, /device:TPU:0, one launch (start us, length us, event | category | flops | bytes accessed | tf_op | source)
XLA Modules:
  0.0 1470.1 jit_solution(8575030756069626106)
XLA Ops:
  8.1 2.1 fusion.14
  12.9 2.8 fusion.93
  16.6 3.1 convolution_convert_fusion.2
  19.8 10.7 all-gather
  30.7 3.6 fusion.95
  34.5 13.1 all-gather.4.cloned.1.call-done
  47.6 4.7 fusion.103
  52.3 3.4 copy-done.5
  57.4 3.5 fusion.104
  62.2 2.1 copy-done.2
  64.3 4.1 fusion.105
  69.7 2.1 copy-done.3
  71.8 3.5 fusion.106
  75.4 3.3 copy-done.4
  80.0 5.6 fusion.30
  85.7 5.4 fusion.31
  91.1 2.2 fusion.32
  96.1 3.3 fusion.81
  99.5 155.0 %all-reduce.8.cloned.1.call-done = f32[512,2048]{1,0:T(8,128)} async-done(((f32[512,2048]{1,0:T(8,128)}), f32[512,2048]{1,0:T(8,128)}) %all-reduce.8.cloned.1.call-update) | async-done | bytes 4194320 | tf_op jit(solution)/shard_map/psum | solution.py:133
  254.6 3.8 multiply_reduce_fusion.6
  259.1 5.0 fusion.108
  264.2 5.0 fusion.107
  269.2 9.1 multiply_convert_fusion.6
  278.3 3.4 fusion.109
  281.7 5.0 convolution_add_fusion.4
  287.2 7.8 convolution_convert_fusion
  296.3 144.5 %all-reduce.12.cloned.1.call-done = f32[512,2048]{1,0:T(8,128)} async-done(((f32[512,2048]{1,0:T(8,128)}), f32[512,2048]{1,0:T(8,128)}) %all-reduce.12.cloned.1.call-update) | async-done | bytes 4194320 | tf_op jit(solution)/shard_map/psum | solution.py:154
  440.9 5.1 multiply_reduce_fusion.4
  446.0 82.8 %all-reduce.10.cloned.1.call-done = bf16[512,2048]{1,0:T(8,128)(2,1)} async-done(((bf16[512,2048]{1,0:T(8,128)(2,1)}), bf16[512,2048]{1,0:T(8,128)(2,1)}) %all-reduce.10.cloned.1.call-update) | async-done | bytes 2097168 | tf_op jit(solution)/shard_map/psum | solution.py:141
  528.8 6.4 convert_add_fusion.1
  538.3 4.6 fusion.38
  545.8 20.1 %multiply_reduce_fusion.2 = (f32[512]{0:T(512)}, f32[512]{0:T(512)}, f32[512]{0:T(512)}, f32[512]{0:T(512)}, f32[512,4096]{1,0:T(8,128)}) fusion(f32[512,4096]{1,0:T(8,128)} %copy-done.3, f32[512]{0:T(512)} %get-tuple-element.64, s32[512]{0:T(512)} %copy-done.47, pred[4096]{0:T(1024)(128)(4,1)S(1)} %bitcast.88, s32[512]{0:T(512)S(1)} %get-tuple-element.31, ...), kind=kOutput, calls=%fused_computation.7 | convolution fusion | flops 578811904 | bytes 68329472 | tf_op jit(solution)/shard_map/dot_general | solution.py:44
  565.9 12.0 multiply_convert_fusion
  578.0 18.2 %multiply_convert_fusion.2 = (bf16[512,4096]{1,0:T(8,128)(2,1)}, bf16[512,4096]{1,0:T(8,128)(2,1)}, bf16[512,4096]{1,0:T(8,128)(2,1)}) fusion(f32[512,4096]{1,0:T(8,128)} %get-tuple-element.61, f32[512]{0:T(512)S(1)} %copy-done.62, f32[512,4096]{1,0:T(8,128)} %copy-done.3, f32[512]{0:T(512)S(1)} %copy-done.55, s32[512]{0:T(512)S(1)} %copy-done.48, ...), kind=kLoop, calls=%fused_computation.6 | loop fusion | flops 39845888 | bytes 62951424 | tf_op jit(solution)/shard_map/convert_element_type | solution.py:184
  596.2 3.1 fusion.77
  604.7 2.5 pad_maximum_fusion
  607.9 6.3 fusion.20
  614.2 6.7 fusion.17
  621.0 6.4 convolution_add_fusion.3
  627.4 3.6 convolution_add_fusion.2
  631.1 2.5 pad_maximum_fusion.1
  633.8 4.3 convolution_multiply_fusion.2
  638.1 3.0 convolution_multiply_fusion.3
  645.2 12.4 reduce-scatter.3.cloned.1.call-done
  658.7 4.1 fusion.110
  662.9 49.7 %reduce-scatter.5.cloned.1.call-done = f32[512,256]{0,1:T(8,128)} async-done(((f32[4096,256]{0,1:T(8,128)}), f32[512,256]{0,1:T(8,128)}) %reduce-scatter.5.cloned.1.call-update) | async-done | bytes 524304 | tf_op jit(solution)/shard_map/reduce_scatter | solution.py:196
  712.6 2.3 fusion.60
  715.3 3.5 add_add_fusion.2
  720.3 7.7 fusion.112
  728.1 6.3 fusion.111
  734.4 6.2 fusion.34
  740.7 3.5 fusion.90
  744.2 3.5 fusion.80
  747.6 2.3 fusion.88
  750.0 2.3 fusion.58
  752.4 121.5 %all-reduce.14.cloned.1.call-done = f32[512,2048]{1,0:T(8,128)} async-done(((f32[512,2048]{1,0:T(8,128)}), f32[512,2048]{1,0:T(8,128)}) %all-reduce.14.cloned.1.call-update) | async-done | bytes 4194320 | tf_op jit(solution)/shard_map/psum | solution.py:218
  873.9 3.5 fusion.11
  877.4 26.1 %all-reduce = (f32[2048]{0:T(1024)}, f32[2048]{0:T(1024)}) all-reduce(f32[2048]{0:T(1024)S(1)} %get-tuple-element.13, f32[2048]{0:T(1024)S(1)} %copy-done.52), channel_id=1, replica_groups=mesh['dp'=8,'tensor'=4] {'dp'}, use_global_device_ids=true, to_apply=%region_23.24 | all-reduce | flops 4096 | bytes 32768 | tf_op jit(solution)/shard_map/psum | solution.py:231
  903.5 6.7 fusion.13
  910.2 513.0 %all-reduce.16.cloned.1.call-done = (f32[2048,512]{1,0:T(8,128)}, f32[2048,256]{1,0:T(8,128)}, f32[2048,256]{1,0:T(8,128)}, f32[512,2048]{1,0:T(8,128)}, f32[204...) async-done(((f32[2048,512]{1,0:T(8,128)}, f32[2048,256]{1,0:T(8,128)}, f32[2048,256]{1,0:T(8,128)}, f32[512,2048]{1,0:T(8,128)}, f32[2048,1408]{1,0:T(8,128)}, ...) | async-done | bytes 47185936 | tf_op jit(solution)/shard_map/psum | solution.py:231
  1423.1 4.8 copy.37
  1433.7 9.4 copy.41
  1443.1 9.4 copy.42
  1452.6 10.8 copy.43
  (231 shorter events, 40.8 us)
Async XLA Ops:
  7.2 89.0 %copy-start = (bf16[512,2048]{1,0:T(8,128)(2,1)S(1)}, bf16[512,2048]{1,0:T(8,128)(2,1)}, u32[]{:S(2)}) copy-start(bf16[512,2048]{1,0:T(8,128)(2,1)} %param.20) | copy-start | bytes 6291460
  7.2 40.4 %all-gather.4.cloned.1.call-start = ((), (), s32[]{:S(2)}) async-start(), calls=%async_computation.2 | async-start | bytes 2359296 | tf_op jit(solution)/shard_map/all_gather | solution.py:115
  10.7 5.9 copy-start.33
  10.7 19.9 %copy-start.45 = (f32[512]{0:T(512)}, f32[512]{0:T(512)S(1)}, u32[]{:S(2)}) copy-start(f32[512]{0:T(512)S(1)} %fusion.83) | copy-start | bytes 6148
  11.5 19.1 %copy-start.43 = (f32[2048]{0:T(1024)}, f32[2048]{0:T(1024)S(1)}, u32[]{:S(2)}) copy-start(f32[2048]{0:T(1024)S(1)} %convert_element_type.116) | copy-start | bytes 24580
  12.9 21.4 %copy-start.21 = (f32[512,64]{0,1:T(8,128)}, f32[512,64]{0,1:T(8,128)S(1)}, u32[]{:S(2)}) copy-start(f32[512,64]{0,1:T(8,128)S(1)} %get-tuple-element.50) | copy-start | bytes 393220
  15.7 4.1 copy-start.66
  16.6 63.4 %all-gather.6.cloned.1.call-start = ((), (), s32[]{:S(2)}) async-start(), calls=%async_computation.3 | async-start | bytes 2359296 | tf_op jit(solution)/shard_map/all_gather | solution.py:116
  19.7 234.9 %all-reduce.8.cloned.1.call-start = ((), (), s32[]{:S(2)}) async-start(), calls=%async_computation.4 | async-start | bytes 8388608 | tf_op jit(solution)/shard_map/psum | solution.py:133
  19.8 49.9 %copy-start.47 = (s32[512]{0:T(512)}, s32[512]{0:T(512)S(1)}, u32[]{:S(2)}) copy-start(s32[512]{0:T(512)S(1)} %iota_add_fusion) | copy-start | bytes 6148
  19.8 515.4 %copy-start.50 = (f32[512]{0:T(512)}, f32[512]{0:T(512)S(1)}, u32[]{:S(2)}) copy-start(f32[512]{0:T(512)S(1)} %get-tuple-element.51) | copy-start | bytes 6148
  34.5 35.2 %copy-start.23 = (bf16[512,4,128]{0,2,1:T(8,128)(2,1)}, bf16[512,4,128]{0,2,1:T(8,128)(2,1)S(1)}, u32[]{:S(2)}) copy-start(bf16[512,4,128]{0,2,1:T(8,128)(2,1)S(1)} %pad_maximum_fusion.3) | copy-start | bytes 1572868
  80.0 5.6 copy-start.17
  80.0 11.1 slice-start
  80.0 13.3 slice-start.2
  85.6 9.8 copy-start.34
  85.6 5.5 slice-start.1
  85.6 7.7 slice-start.3
  91.1 4.3 copy-start.36
  99.5 341.4 %all-reduce.12.cloned.1.call-start = ((), (), s32[]{:S(2)}) async-start(), calls=%async_computation.6 | async-start | bytes 8388608 | tf_op jit(solution)/shard_map/psum | solution.py:154
  254.6 4.3 slice-start.8
  254.6 4.5 slice-start.9
  258.4 5.7 copy-start.6
  258.4 5.7 slice-start.6
  259.1 5.0 copy-start.27
  259.1 5.0 slice-start.7
  264.2 5.0 copy-start.25
  286.8 242.0 %all-reduce.10.cloned.1.call-start = ((), (), s32[]{:S(2)}) async-start(), calls=%async_computation.5 | async-start | bytes 4194304 | tf_op jit(solution)/shard_map/psum | solution.py:141
  295.1 362.5 %reduce-scatter.3.cloned.1.call-start = ((), (), s32[]{:S(2)}) async-start(), calls=%async_computation.7 | async-start | bytes 4718592 | tf_op jit(solution)/shard_map/reduce_scatter | solution.py:195
  535.2 7.7 copy-start.8
  565.9 12.1 copy-start.48
  565.9 12.1 copy-start.53
  565.9 12.1 copy-start.55
  565.9 12.1 copy-start.57
  565.9 12.1 copy-start.62
  565.9 12.1 copy-start.63
  565.9 12.1 copy-start.64
  578.0 18.2 %copy-start.24 = (bf16[512,4,128]{0,2,1:T(8,128)(2,1)S(1)}, bf16[512,4,128]{0,2,1:T(8,128)(2,1)}, u32[]{:S(2)}) copy-start(bf16[512,4,128]{0,2,1:T(8,128)(2,1)} %copy-done.23) | copy-start | bytes 1572868
  607.3 6.9 copy-start.54
  607.3 105.3 %reduce-scatter.5.cloned.1.call-start = ((), (), s32[]{:S(2)}) async-start(), calls=%async_computation.8 | async-start | bytes 4718592 | tf_op jit(solution)/shard_map/reduce_scatter | solution.py:196
  607.9 19.5 %slice-start.4 = ((s8[8388608]{0:T(1024)(128)(4,1)}), s8[4194304]{0:T(1024)(128)(4,1)S(1)}, s32[]{:S(2)}) async-start(s8[8388608]{0:T(1024)(128)(4,1)} %bitcast.53), calls=%async_computation.15 | async-start | bytes 8388608
  614.2 6.8 copy-start.56
  614.2 13.2 slice-start.5
  621.0 6.4 copy-start.59
  633.6 240.3 %all-reduce.14.cloned.1.call-start = ((), (), s32[]{:S(2)}) async-start(), calls=%async_computation.9 | async-start | bytes 8388608 | tf_op jit(solution)/shard_map/psum | solution.py:218
  633.8 4.3 copy-start.13
  633.8 7.3 copy-start.68
  658.7 56.2 %copy-start.31 = (bf16[2048,512]{1,0:T(8,128)(2,1)S(1)}, bf16[2048,512]{1,0:T(8,128)(2,1)}, u32[]{:S(2)}) copy-start(bf16[2048,512]{1,0:T(8,128)(2,1)} %param.17) | copy-start | bytes 6291460
  718.7 704.4 %all-reduce.16.cloned.1.call-start = ((), (), s32[]{:S(2)}) async-start(), calls=%async_computation.10 | async-start | bytes 94371840 | tf_op jit(solution)/shard_map/psum | solution.py:231
  720.3 7.7 copy-start.70
  728.0 6.3 copy-start.26
  728.0 6.3 copy-start.51
  728.0 6.3 copy-start.72
  734.3 6.3 copy-start.7
  734.4 6.3 copy-start.44
  734.4 6.2 copy-start.46
  740.6 3.6 copy-start.9
  740.6 3.5 copy-start.35
  752.3 125.0 %copy-start.52 = (f32[2048]{0:T(1024)S(1)}, f32[2048]{0:T(1024)}, u32[]{:S(2)}) copy-start(f32[2048]{0:T(1024)} %get-tuple-element.11) | copy-start | bytes 24580
  752.3 151.1 %copy-start.61 = (f32[512]{0:T(512)S(1)}, f32[512]{0:T(512)}, u32[]{:S(2)}) copy-start(f32[512]{0:T(512)} %copy-done.60) | copy-start | bytes 6148
  1423.1 4.8 copy-start.30
  1423.1 6.1 copy-start.29
  1428.0 3.7 copy-start.20
  1452.6 10.8 copy-start.1
  (28 other events, 68.4 us)
Sparse Core Ops, SparseCore 0:
  16.7 30.8 all-gather.3
  50.0 27.7 all-gather.5
  99.6 154.9 all-reduce.7
  286.9 153.9 all-reduce.11
  443.7 85.0 all-reduce.9
  607.4 50.1 reduce-scatter.2
  661.5 51.0 reduce-scatter.4
  718.9 154.9 all-reduce.13
  880.2 542.9 all-reduce.15
where the time goes:
time: 1470 us
  waiting for transfers between devices  1090 us (74%)
  matrix products  188 us (13%)
  other arithmetic  75.1 us (5%)
  local copies, waits for them, and re-layouts  61.1 us (4%)
  blocking collectives  36.8 us (3%)
  between operations  15.1 us (1%)
    psum x1, waiting for transfers between devices, on_device(): lax.psum((grad_gain_one, grad_w_query, grad_w_key, grad_w_value, grad_w_o...  513 us
    psum x1, waiting for transfers between devices, on_device(): lax.psum(jnp.dot(attended, w_out, preferred_element_type=jnp.float32), 't...  155 us
    psum x1, waiting for transfers between devices, on_device(): lax.psum(right_trans(d_gate, w_gate) + right_trans(d_up, w_up), 'tensor')  145 us
    psum x1, waiting for transfers between devices, on_device(): d_normed = lax.psum(d_normed_part, 'tensor')  122 us
    psum x1, waiting for transfers between devices, on_device(): lax.psum(jnp.dot(hidden, w_down, preferred_element_type=jnp.float32).asty...  82.8 us
    dot_general x15, matrix products, right_trans(): lax.dot_general(left, right, (((1,), (1,)), ((), ())), preferred_element_...  71.8 us
    unnamed x176, local copies, waits for them, and re-layouts  61.1 us
    dot_general x15, matrix products, left_trans(): lax.dot_general(left, right, (((0,), (0,)), ((), ())), preferred_element_...  60.4 us
  transfers between devices with their start and end apart: 9, of which 8 were waited for; matrix products, arithmetic and copies ran while one was open for 9% of the time, Pallas kernels for 0%

commit v1 on v0

--- a/solution.py
+++ b/solution.py
@@ -111,11 +111,13 @@
         raw_scores = right_trans(query_part, key_part) * score_scale
         return jnp.where(allowed, raw_scores, MASKED_SCORE)
 
-    all_keys, all_values, all_alive = (
-        lax.all_gather(key_low, "dp", axis=0, tiled=True),
-        lax.all_gather(value_low, "dp", axis=0, tiled=True),
-        lax.all_gather(alive_low, "dp", axis=0, tiled=True),
-    )
+    kv_width = local_groups * HEAD_DIM
+    all_kv = lax.all_gather(
+        jnp.concatenate([key_low, value_low], axis=1), "dp", axis=0, tiled=True
+    )
+    all_keys = all_kv[:, :kv_width]
+    all_values = all_kv[:, kv_width:]
+    all_alive = lax.all_gather(alive_low, "dp", axis=0, tiled=True)
     allowed_fwd = allowed_of(all_alive)
     mixed_parts = []
     lse_parts = []
@@ -130,7 +132,9 @@
         value_part = all_values[:, group_index * HEAD_DIM : (group_index + 1) * HEAD_DIM]
         mixed_parts.append(jnp.dot(probs_low, value_part, preferred_element_type=jnp.float32))
     attended = jnp.concatenate(mixed_parts, axis=1).astype(jnp.bfloat16)
-    branch = lax.psum(jnp.dot(attended, w_out, preferred_element_type=jnp.float32), "tensor")
+    branch = lax.psum(
+        jnp.dot(attended, w_out, preferred_element_type=jnp.float32).astype(jnp.bfloat16), "tensor"
+    ).astype(jnp.float32)
     middle = source + keep_rows * branch
     normed_two_full, norm_two_back = jax.vjp(rms_norm, middle, gain_two.astype(jnp.float32))
     normed_two = normed_two_full.astype(jnp.bfloat16)
@@ -151,18 +155,16 @@
     d_up = d_up_full.astype(jnp.bfloat16)
     grad_w_gate = left_trans(normed_two, d_gate)
     grad_w_up = left_trans(normed_two, d_up)
-    d_normed_two = lax.psum(right_trans(d_gate, w_gate) + right_trans(d_up, w_up), "tensor")
+    d_normed_two = lax.psum(
+        (right_trans(d_gate, w_gate) + right_trans(d_up, w_up)).astype(jnp.bfloat16), "tensor"
+    ).astype(jnp.float32)
     d_middle_norm, grad_gain_two = norm_two_back(d_normed_two)
     grad_middle = grad_out + d_middle_norm
     d_branch = (keep_rows * grad_middle).astype(jnp.bfloat16)
     grad_w_out = left_trans(attended, d_branch)
     d_attended = right_trans(d_branch, w_out).astype(jnp.bfloat16)
-    back_keys, back_values, back_alive = (
-        lax.all_gather(key_low, "dp", axis=0, tiled=True),
-        lax.all_gather(value_low, "dp", axis=0, tiled=True),
-        lax.all_gather(alive_low, "dp", axis=0, tiled=True),
-    )
-    allowed_back = allowed_of(back_alive)
+    back_keys, back_values = all_keys, all_values
+    allowed_back = allowed_fwd
     d_query_parts = []
     d_key_parts = [
         jnp.zeros((length, HEAD_DIM), jnp.float32) for group_index in range(local_groups)
@@ -191,10 +193,14 @@
         d_value_parts[group_index] = d_value_parts[group_index] + left_trans(probs_low, d_out_part)
     d_key_all = jnp.concatenate(d_key_parts, axis=1)
     d_value_all = jnp.concatenate(d_value_parts, axis=1)
-    d_key_own, d_value_own = (
-        lax.psum_scatter(d_key_all, "dp", scatter_dimension=0, tiled=True),
-        lax.psum_scatter(d_value_all, "dp", scatter_dimension=0, tiled=True),
-    )
+    d_kv_own = lax.psum_scatter(
+        jnp.concatenate([d_key_all, d_value_all], axis=1).astype(jnp.bfloat16),
+        "dp",
+        scatter_dimension=0,
+        tiled=True,
+    ).astype(jnp.float32)
+    d_key_own = d_kv_own[:, :kv_width]
+    d_value_own = d_kv_own[:, kv_width:]
     d_queries = jnp.concatenate(d_query_parts, axis=1).reshape(row_count, local_heads, HEAD_DIM)
     d_query_low = (
         rotate(d_queries, cos_table, -sin_table)
@@ -215,33 +221,30 @@
         + right_trans(d_key_low, w_key)
         + right_trans(d_value_low, w_value)
     )
-    d_normed = lax.psum(d_normed_part, "tensor")
+    d_normed = lax.psum(d_normed_part.astype(jnp.bfloat16), "tensor").astype(jnp.float32)
     d_source_norm, grad_gain_one = norm_one_back(d_normed)
     grad_input = grad_middle + d_source_norm
+    grad_gain_one, grad_gain_two = lax.psum((grad_gain_one, grad_gain_two), "dp")
     (
-        grad_gain_one,
         grad_w_query,
         grad_w_key,
         grad_w_value,
         grad_w_out,
-        grad_gain_two,
         grad_w_gate,
         grad_w_up,
         grad_w_down,
-    ) = lax.psum(
-        (
-            grad_gain_one,
+    ) = [
+        lax.psum(grad.astype(jnp.bfloat16), "dp").astype(jnp.float32)
+        for grad in (
             grad_w_query,
             grad_w_key,
             grad_w_value,
             grad_w_out,
-            grad_gain_two,
             grad_w_gate,
             grad_w_up,
             grad_w_down,
-        ),
-        "dp",
-    )
+        )
+    ]
     return (
         output,
         grad_input,

time: 1470 us -> 964 us (0.66)
  waiting for transfers between devices: 1090 us -> 614 us
  local copies, waits for them, and re-layouts: 61.1 us -> 13 us
  other arithmetic: 75.1 us -> 100 us
    psum x4 -> x3, waiting for transfers between devices: 934 us -> 430 us  [the longest x1 259 us: on_device(): lax.psum(grad.astype(jnp.bfloat16), 'dp').astype(jnp.float32)]
    unnamed x176 -> x189, local copies, waits for them, and re-layouts: 61.1 us -> 12 us
    psum x1, waiting for transfers between devices: 82.8 us -> 126 us  [on_device(): lax.psum(jnp.dot(hidden, w_down, preferred_element_type=jnp.float32).asty...]
    reduce_scatter x2 -> x1, waiting for transfers between devices: 62.1 us -> 32.3 us  [on_device(): lax.psum_scatter(jnp.concatenate([d_key_all, d_value_all], axis=1).astype...]
    convert_element_type x0 -> x7, other arithmetic: none -> 28 us  [on_device(): lax.psum(grad.astype(jnp.bfloat16), 'dp').astype(jnp.float32)]
  transfers between devices with their start and end apart: 9 -> 6, of which waited for: 8 -> 6; matrix products, arithmetic and copies ran while one was open for 9% -> 6% of each run, Pallas kernels for 0% -> 0%
where the time goes in v1:
time: 964 us; the launch traced here: 961 us
  waiting for transfers between devices  614 us (64%)
  matrix products  181 us (19%)
  other arithmetic  100 us (10%)
  blocking collectives  36.8 us (4%)
  between operations  15.7 us (2%)
  local copies, waits for them, and re-layouts  13 us (1%)
    psum x1, waiting for transfers between devices, on_device(): lax.psum(grad.astype(jnp.bfloat16), 'dp').astype(jnp.float32)  259 us
    psum x1, waiting for transfers between devices, on_device(): lax.psum(jnp.dot(hidden, w_down, preferred_element_type=jnp.float32).asty...  126 us
    psum x1, waiting for transfers between devices, on_device(): lax.psum(jnp.dot(attended, w_out, preferred_element_type=jnp.float32).ast...  86.2 us
    dot_general x15, matrix products, right_trans(): lax.dot_general(left, right, (((1,), (1,)), ((), ())), preferred_element_...  84.3 us
    psum x1, waiting for transfers between devices, on_device(): lax.psum((right_trans(d_gate, w_gate) + right_trans(d_up, w_up)).astype(j...  84.1 us
    dot_general x15, matrix products, left_trans(): lax.dot_general(left, right, (((0,), (0,)), ((), ())), preferred_element_...  49.7 us
    reduce_scatter x1, waiting for transfers between devices, on_device(): lax.psum_scatter(jnp.concatenate([d_key_all, d_value_all], axis=1).astype...  32.3 us
    convert_element_type x2, other arithmetic, on_device(): d_scores = (probs * (d_probs - row_delta)).astype(jnp.bfloat16)  28 us
  transfers between devices with their start and end apart: 6, of which 6 were waited for; matrix products, arithmetic and copies ran while one was open for 6% of the time, Pallas kernels for 0%

profile of v1, /device:TPU:0, one launch (start us, length us, event | category | flops | bytes accessed | tf_op | source)
XLA Modules:
  0.0 960.6 jit_solution(8947270044734989790)
XLA Ops:
  8.2 2.2 fusion.22
  11.2 3.6 fusion.95
  19.2 10.6 %all-gather = bf16[8,1,512]{2,1,0:T(2,128)(2,1)S(1)} all-gather(bf16[1,1,512]{2,1,0:T(2,128)(2,1)S(1)} %reshape.237), channel_id=1, replica_groups=mesh['dp'=8,'tensor'=4] {'dp'}, dimensions={0}, use_global_device_ids=true | all-gather | bytes 9216 | tf_op jit(solution)/shard_map/all_gather | solution.py:120
  29.9 3.7 fusion.97
  33.9 25.4 %all-gather.3.cloned.1.call-done = bf16[4096,512]{0,1:T(8,128)(2,1)} async-done(((bf16[512,512]{0,1:T(8,128)(2,1)}), bf16[4096,512]{0,1:T(8,128)(2,1)}) %all-gather.3.cloned.1.call-update) | async-done | bytes 4194320 | tf_op jit(solution)/shard_map/all_gather | solution.py:115
  59.3 4.7 fusion.108
  65.3 5.5 fusion.107
  72.1 6.0 fusion.106
  79.4 7.7 fusion.105
  87.1 4.6 fusion.5
  91.8 3.2 fusion.41
  95.0 3.3 fusion.40
  98.3 1.9 fusion.39
  100.7 1.8 fusion.38
  103.1 2.6 convolution_convert_fusion.5
  105.8 86.2 %all-reduce.8.cloned.1.call-done = bf16[512,2048]{1,0:T(8,128)(2,1)} async-done(((bf16[512,2048]{1,0:T(8,128)(2,1)}), bf16[512,2048]{1,0:T(8,128)(2,1)}) %all-reduce.8.cloned.1.call-update) | async-done | bytes 2097168 | tf_op jit(solution)/shard_map/psum | solution.py:135
  192.1 3.3 multiply_reduce_fusion.4
  196.5 7.1 fusion.109
  203.7 5.0 fusion.110
  208.7 9.4 multiply_convert_fusion.6
  218.1 4.9 fusion.111
  223.0 4.7 add_convert_fusion.1
  229.0 84.1 %all-reduce.10.cloned.1.call-done = bf16[512,2048]{1,0:T(8,128)(2,1)} async-done(((bf16[512,2048]{1,0:T(8,128)(2,1)}), bf16[512,2048]{1,0:T(8,128)(2,1)}) %all-reduce.10.cloned.1.call-update) | async-done | bytes 2097168 | tf_op jit(solution)/shard_map/psum | solution.py:158
  313.1 5.5 fusion.19
  318.6 4.1 convert_add_fusion.1
  322.7 2.0 copy-done.10
  326.1 4.9 fusion.28
  331.1 4.9 fusion.25
  336.0 4.6 fusion.45
  340.5 4.5 fusion.47
  345.1 4.6 fusion.57
  349.8 20.7 %multiply_reduce_fusion.2 = (f32[512]{0:T(512)S(1)}, f32[512]{0:T(512)S(1)}, f32[512]{0:T(512)S(1)}, f32[512]{0:T(512)S(1)}, f32[512,4096]{1,0:T(8,128)}) fusion(f32[512,4096]{1,0:T(8,128)S(1)} %bitcast.51, f32[512]{0:T(512)S(1)} %copy-done.57, s32[512]{0:T(512)S(1)} %copy-done.54, pred[4096]{0:T(1024)(128)(4,1)S(1)} %bitcast.97, s32[512]{0:T(512)S(1)} %copy-done.51, ...), kind=kOutput, calls=%fused_computation.7 | convolution fusion | flops 578811904 | bytes 68329472 | tf_op jit(solution)/shard_map/dot_general | solution.py:44
  370.5 9.8 %multiply_convert_fusion = bf16[512,4096]{1,0:T(8,128)(2,1)} fusion(f32[512,4096]{1,0:T(8,128)} %fusion.45, f32[512]{0:T(512)S(1)} %get-tuple-element.18, f32[512,4096]{1,0:T(8,128)} %get-tuple-element.54, f32[512]{0:T(512)S(1)} %copy-done.65, s32[512]{0:T(512)S(1)} %copy-done.54, pred[4096]{0:T(1024)(128)(4,1)S(1)} %bitcast.98, s32[512]{0:T(512)S(1)} %copy-done.51, ...), kind=kLoop, calls=%fused_computation | loop fusion | flops 18874368 | bytes 21000192 | tf_op jit(solution)/shard_map/convert_element_type | solution.py:186
  380.3 18.2 %multiply_convert_fusion.2 = (bf16[512,4096]{1,0:T(8,128)(2,1)}, bf16[512,4096]{1,0:T(8,128)(2,1)}, bf16[512,4096]{1,0:T(8,128)(2,1)}) fusion(f32[512,4096]{1,0:T(8,128)} %get-tuple-element.61, f32[512]{0:T(512)S(1)} %get-tuple-element.15, f32[512,4096]{1,0:T(8,128)S(1)} %bitcast.51, f32[512]{0:T(512)S(1)} %copy-done.57, s32[512]{0:T(512)S(1)} %copy-done.54, ...), kind=kLoop, calls=%fused_computation.6 | loop fusion | flops 39845888 | bytes 62951424 | tf_op jit(solution)/shard_map/convert_element_type | solution.py:186
  398.6 3.1 fusion.83
  403.4 3.7 fusion.12
  407.1 3.7 fusion.13
  413.9 2.2 pad_maximum_fusion
  417.5 7.6 convolution_convert_fusion.6
  425.1 1.5 convolution_multiply_fusion
  427.7 1.5 convolution_multiply_fusion.1
  430.0 1.5 convolution_multiply_fusion.2
  432.2 1.5 convolution_multiply_fusion.3
  434.1 32.3 %reduce-scatter.2.cloned.1.call-done = bf16[512,512]{0,1:T(8,128)(2,1)} async-done(((bf16[4096,512]{0,1:T(8,128)(2,1)}), bf16[512,512]{0,1:T(8,128)(2,1)}) %reduce-scatter.2.cloned.1.call-update) | async-done | bytes 524304 | tf_op jit(solution)/shard_map/reduce_scatter | solution.py:196
  467.6 2.1 fusion.112
  471.3 2.7 add_convert_fusion
  474.1 1.5 copy-done.31
  475.6 7.0 convolution_convert_fusion.1
  482.6 5.3 convolution_convert_fusion.2
  488.0 5.2 convolution_convert_fusion
  493.2 2.8 convolution_convert_fusion.4
  496.1 2.7 convolution_convert_fusion.3
  498.7 2.0 convolution_convert_fusion.8
  500.7 2.0 convolution_convert_fusion.7
  502.7 126.5 %all-reduce.14.cloned.1.call-done = (bf16[512,2048]{1,0:T(8,128)(2,1)}, bf16[512,2048]{1,0:T(8,128)(2,1)}) async-done(((bf16[512,2048]{1,0:T(8,128)(2,1)}, bf16[512,2048]{1,0:T(8,128)(2,1)}), (bf16[512,2048]{1,0:T(8,128)(2,1)}, bf16[512,2048]{1,0:T(8,128)(2,1)})) %all-reduce.14.cloned.1.call-update) | async-done | bytes 4194320 | tf_op jit(solution)/shard_map/psum | solution.py:145
  629.2 3.3 fusion.20
  632.5 26.2 %all-reduce = (f32[2048]{0:T(1024)}, f32[2048]{0:T(1024)}) all-reduce(f32[2048]{0:T(1024)S(1)} %get-tuple-element.13, f32[2048]{0:T(1024)S(1)} %copy-done.56), channel_id=1, replica_groups=mesh['dp'=8,'tensor'=4] {'dp'}, use_global_device_ids=true, to_apply=%region_22.23 | all-reduce | flops 4096 | bytes 32768 | tf_op jit(solution)/shard_map/psum | solution.py:227
  658.8 7.1 fusion.21
  665.8 259.4 %all-reduce.12.cloned.1.call-done = (bf16[2048,512]{1,0:T(8,128)(2,1)}, bf16[2048,256]{1,0:T(8,128)(2,1)}, bf16[2048,256]{1,0:T(8,128)(2,1)}, bf16[512,2048]{1,0...) async-done(((bf16[2048,512]{1,0:T(8,128)(2,1)}, bf16[2048,256]{1,0:T(8,128)(2,1)}, bf16[2048,256]{1,0:T(8,128)(2,1)}, ...) | async-done | bytes 23592976 | tf_op jit(solution)/shard_map/psum | solution.py:237
  925.2 8.6 convert_element_type.223
  933.8 5.2 convert_element_type.225
  939.0 6.0 convert_element_type.227
  945.0 2.6 convert_element_type.215
  947.6 2.7 convert_element_type.221
  (247 shorter events, 29.8 us)
Async XLA Ops:
  7.2 96.0 %copy-start = (bf16[512,2048]{1,0:T(8,128)(2,1)S(1)}, bf16[512,2048]{1,0:T(8,128)(2,1)}, u32[]{:S(2)}) copy-start(bf16[512,2048]{1,0:T(8,128)(2,1)} %param.20) | copy-start | bytes 6291460
  7.2 7.6 copy-start.37
  7.2 52.1 %all-gather.3.cloned.1.call-start = ((), (), s32[]{:S(2)}) async-start(), calls=%async_computation.1 | async-start | bytes 4718592 | tf_op jit(solution)/shard_map/all_gather | solution.py:115
  8.2 6.5 copy-start.2
  10.5 5.3 copy-start.67
  10.5 19.4 %copy-start.63 = (f32[512]{0:T(512)}, f32[512]{0:T(512)S(1)}, u32[]{:S(2)}) copy-start(f32[512]{0:T(512)S(1)} %fusion.87) | copy-start | bytes 6148
  11.2 18.7 %copy-start.48 = (f32[2048]{0:T(1024)}, f32[2048]{0:T(1024)S(1)}, u32[]{:S(2)}) copy-start(f32[2048]{0:T(1024)S(1)} %convert_element_type.176) | copy-start | bytes 24580
  14.8 4.4 copy-start.70
  15.8 315.2 %copy-start.50 = (s32[512]{0:T(512)}, s32[512]{0:T(512)S(1)}, u32[]{:S(2)}) copy-start(s32[512]{0:T(512)S(1)} %get-tuple-element.31) | copy-start | bytes 6148
  17.0 16.6 %copy-start.23 = (f32[512,64]{0,1:T(8,128)}, f32[512,64]{0,1:T(8,128)S(1)}, u32[]{:S(2)}) copy-start(f32[512,64]{0,1:T(8,128)S(1)} %get-tuple-element.50) | copy-start | bytes 393220
  19.1 173.0 %all-reduce.8.cloned.1.call-start = ((), (), s32[]{:S(2)}) async-start(), calls=%async_computation.2 | async-start | bytes 4194304 | tf_op jit(solution)/shard_map/psum | solution.py:135
  29.9 301.1 %copy-start.53 = (s32[512]{0:T(512)}, s32[512]{0:T(512)S(1)}, u32[]{:S(2)}) copy-start(s32[512]{0:T(512)S(1)} %iota_add_fusion) | copy-start | bytes 6148
  33.9 45.5 %copy-start.25 = (bf16[512,4,128]{0,2,1:T(8,128)(2,1)}, bf16[512,4,128]{0,2,1:T(8,128)(2,1)S(1)}, u32[]{:S(2)}) copy-start(bf16[512,4,128]{0,2,1:T(8,128)(2,1)S(1)} %pad_maximum_fusion.2) | copy-start | bytes 1572868
  64.0 27.7 %copy-start.7 = (f32[512,4096]{1,0:T(8,128)}, f32[512,4096]{1,0:T(8,128)S(1)}, u32[]{:S(2)}) copy-start(f32[512,4096]{1,0:T(8,128)S(1)} %get-tuple-element.60) | copy-start | bytes 25165828
  70.8 24.1 %copy-start.6 = (f32[512,4096]{1,0:T(8,128)}, f32[512,4096]{1,0:T(8,128)S(1)}, u32[]{:S(2)}) copy-start(f32[512,4096]{1,0:T(8,128)S(1)} %get-tuple-element.58) | copy-start | bytes 25165828
  78.1 20.2 %copy-start.8 = (f32[512,4096]{1,0:T(8,128)}, f32[512,4096]{1,0:T(8,128)S(1)}, u32[]{:S(2)}) copy-start(f32[512,4096]{1,0:T(8,128)S(1)} %get-tuple-element.56) | copy-start | bytes 25165828
  94.9 7.5 copy-start.40
  95.0 5.3 slice-start.6
  98.3 4.2 copy-start.42
  105.8 207.3 %all-reduce.10.cloned.1.call-start = ((), (), s32[]{:S(2)}) async-start(), calls=%async_computation.3 | async-start | bytes 4194304 | tf_op jit(solution)/shard_map/psum | solution.py:158
  195.6 8.1 slice-start.14
  196.5 7.1 copy-start.30
  196.5 7.1 slice-start.15
  203.6 5.0 copy-start.32
  203.7 14.4 %slice-start.12 = ((s8[5767168]{0:T(1024)(128)(4,1)}), s8[4194304]{0:T(1024)(128)(4,1)S(1)}, s32[]{:S(2)}) async-start(s8[5767168]{0:T(1024)(128)(4,1)} %bitcast.103), calls=%async_computation.19 | async-start | bytes 8388608
  208.7 9.4 slice-start.13
  218.1 5.0 copy-start.76
  227.8 238.7 %reduce-scatter.2.cloned.1.call-start = ((), (), s32[]{:S(2)}) async-start(), calls=%async_computation.4 | async-start | bytes 4718592 | tf_op jit(solution)/shard_map/reduce_scatter | solution.py:196
  228.4 97.6 %copy-start.59 = (f32[512]{0:T(512)}, f32[512]{0:T(512)S(1)}, u32[]{:S(2)}) copy-start(f32[512]{0:T(512)S(1)} %get-tuple-element.65) | copy-start | bytes 6148
  229.0 102.0 %copy-start.61 = (f32[512]{0:T(512)}, f32[512]{0:T(512)S(1)}, u32[]{:S(2)}) copy-start(f32[512]{0:T(512)S(1)} %get-tuple-element.63) | copy-start | bytes 6148
  313.1 5.5 copy-start.4
  313.1 13.0 %slice-start.2 = ((s8[8388608]{0:T(1024)(128)(4,1)}), s8[4194304]{0:T(1024)(128)(4,1)S(1)}, s32[]{:S(2)}) async-start(s8[8388608]{0:T(1024)(128)(4,1)} %bitcast.52), calls=%async_computation.9 | async-start | bytes 8388608
  318.6 7.5 slice-start.3
  324.7 6.3 slice-start.4
  326.1 5.0 slice-start.5
  331.0 4.9 copy-start.21
  340.5 9.2 slice-start
  345.1 4.7 slice-start.1
  345.1 4.7 copy-start.51
  345.1 4.7 copy-start.54
  345.1 4.7 copy-start.57
  345.1 4.7 copy-start.60
  345.1 4.7 copy-start.62
  345.1 4.7 copy-start.65
  380.3 18.2 %copy-start.26 = (bf16[512,4,128]{0,2,1:T(8,128)(2,1)S(1)}, bf16[512,4,128]{0,2,1:T(8,128)(2,1)}, u32[]{:S(2)}) copy-start(bf16[512,4,128]{0,2,1:T(8,128)(2,1)} %copy-done.25) | copy-start | bytes 1572868
  402.0 5.1 slice-start.8
  416.2 213.0 %all-reduce.14.cloned.1.call-start = ((), (), s32[]{:S(2)}) async-start(), calls=%async_computation.6 | async-start | bytes 8388608 | tf_op jit(solution)/shard_map/psum | solution.py:145
  417.5 7.6 copy-start.18
  417.5 7.6 copy-start.22
  474.1 451.1 %all-reduce.12.cloned.1.call-start = ((), (), s32[]{:S(2)}) async-start(), calls=%async_computation.5 | async-start | bytes 47185920 | tf_op jit(solution)/shard_map/psum | solution.py:237
  475.6 7.0 copy-start.75
  482.6 5.3 copy-start.33
  482.6 5.3 copy-start.74
  488.0 5.2 copy-start.5
  488.0 5.2 copy-start.49
  488.0 5.2 copy-start.64
  502.7 129.8 %copy-start.56 = (f32[2048]{0:T(1024)S(1)}, f32[2048]{0:T(1024)}, u32[]{:S(2)}) copy-start(f32[2048]{0:T(1024)} %get-tuple-element.11) | copy-start | bytes 24580
  502.7 156.0 %copy-start.68 = (f32[512]{0:T(512)S(1)}, f32[512]{0:T(512)}, u32[]{:S(2)}) copy-start(f32[512]{0:T(512)} %copy-done.67) | copy-start | bytes 6148
  925.2 8.6 copy-start.19
  925.2 13.8 %slice-start.10 = ((s8[5767168]{0:T(1024)(128)(4,1)}), s8[4194304]{0:T(1024)(128)(4,1)S(1)}, s32[]{:S(2)}) async-start(s8[5767168]{0:T(1024)(128)(4,1)} %bitcast.60), calls=%async_computation.17 | async-start | bytes 8388608
  933.8 5.2 slice-start.11
  939.0 6.0 copy-start.29
  947.6 4.2 copy-start.35
  947.6 5.6 copy-start.1
  (35 other events, 83.8 us)
Sparse Core Ops, SparseCore 0:
  19.2 40.0 all-gather.2
  105.9 86.1 all-reduce.7
  227.9 85.1 all-reduce.9
  416.3 50.0 reduce-scatter.1
  474.2 154.9 all-reduce.13
  635.4 289.7 all-reduce.11

commit v2 on v1

--- a/solution.py
+++ b/solution.py
@@ -44,6 +44,48 @@
     return lax.dot_general(
         left, right, (((1,), (1,)), ((), ())), preferred_element_type=jnp.float32
     )
+
+
+def partner_perm(axis_size, mask):
+    return [(index, index ^ mask) for index in range(axis_size)]
+
+
+def permute_sum(parts, dims, axis):
+    size = lax.axis_size(axis)
+    steps = size.bit_length() - 1
+    assert 1 << steps == size
+    me = lax.axis_index(axis)
+    pieces = list(parts)
+    for step in range(steps):
+        bit = (me >> step) & 1
+        keep, send = [], []
+        for piece, dim in zip(pieces, dims):
+            half = piece.shape[dim] // 2
+            keep.append(lax.dynamic_slice_in_dim(piece, bit * half, half, axis=dim))
+            send.append(
+                lax.dynamic_slice_in_dim(piece, (1 - bit) * half, half, axis=dim).astype(jnp.bfloat16)
+            )
+        got = lax.ppermute(send, axis, partner_perm(size, 1 << step))
+        pieces = [mine + theirs.astype(jnp.float32) for mine, theirs in zip(keep, got)]
+    pieces = [piece.astype(jnp.bfloat16) for piece in pieces]
+    for step in reversed(range(steps)):
+        first = ((me >> step) & 1) == 0
+        got = lax.ppermute(pieces, axis, partner_perm(size, 1 << step))
+        pieces = [
+            jnp.concatenate(
+                [jnp.where(first, mine, theirs), jnp.where(first, theirs, mine)], axis=dim
+            )
+            for mine, theirs, dim in zip(pieces, got, dims)
+        ]
+    return [piece.astype(jnp.float32) for piece in pieces]
+
+
+def permute_allsum(value, axis):
+    size = lax.axis_size(axis)
+    steps = size.bit_length() - 1
+    for step in range(steps):
+        value = value + lax.ppermute(value, axis, partner_perm(size, 1 << step))
+    return value
 
 
 def on_device(
@@ -224,27 +266,15 @@
     d_normed = lax.psum(d_normed_part.astype(jnp.bfloat16), "tensor").astype(jnp.float32)
     d_source_norm, grad_gain_one = norm_one_back(d_normed)
     grad_input = grad_middle + d_source_norm
-    grad_gain_one, grad_gain_two = lax.psum((grad_gain_one, grad_gain_two), "dp")
-    (
-        grad_w_query,
-        grad_w_key,
-        grad_w_value,
-        grad_w_out,
-        grad_w_gate,
-        grad_w_up,
-        grad_w_down,
-    ) = [
-        lax.psum(grad.astype(jnp.bfloat16), "dp").astype(jnp.float32)
-        for grad in (
-            grad_w_query,
-            grad_w_key,
-            grad_w_value,
-            grad_w_out,
-            grad_w_gate,
-            grad_w_up,
-            grad_w_down,
-        )
-    ]
+    grad_gain_one = permute_allsum(grad_gain_one, "dp")
+    grad_gain_two = permute_allsum(grad_gain_two, "dp")
+    grad_w_gate, grad_w_up, grad_w_down = permute_sum(
+        [grad_w_gate, grad_w_up, grad_w_down], [0, 0, 1], "dp"
+    )
+    (grad_w_out,) = permute_sum([grad_w_out], [1], "dp")
+    grad_w_query, grad_w_key, grad_w_value = permute_sum(
+        [grad_w_query, grad_w_key, grad_w_value], [0, 0, 0], "dp"
+    )
     return (
         output,
         grad_input,

time: 964 us -> 924 us (0.959)
  waiting for transfers between devices: 614 us -> 494 us
  other arithmetic: 100 us -> 148 us
  starting transfers between devices: 0.25 us -> 42.3 us
  blocking collectives: 36.8 us -> 10.9 us
  local copies, waits for them, and re-layouts: 13 us -> 35.2 us
    psum x1 -> x0, waiting for transfers between devices: 259 us -> none  [on_device(): lax.psum(grad.astype(jnp.bfloat16), 'dp').astype(jnp.float32)]
    ppermute x0 -> x48, waiting for transfers between devices: none -> 244 us  [the longest x21 123 us: permute_sum(): got = lax.ppermute(pieces, axis, partner_perm(size, 1 << step))]
    psum x1, waiting for transfers between devices: 126 us -> 82.8 us  [on_device(): lax.psum(jnp.dot(hidden, w_down, preferred_element_type=jnp.float32).asty...]
    ppermute x0 -> x48, starting transfers between devices: none -> 41.7 us  [the longest x21 18.1 us: permute_sum(): got = lax.ppermute(send, axis, partner_perm(size, 1 << step))]
    reduce_scatter x1, waiting for transfers between devices: 32.3 us -> 0.01 us  [on_device(): lax.psum_scatter(jnp.concatenate([d_key_all, d_value_all], axis=1).astype...]
    psum x1, waiting for transfers between devices: 84.1 us -> 55.2 us  [on_device(): lax.psum((right_trans(d_gate, w_gate) + right_trans(d_up, w_up)).astype(j...]
    psum x1 -> x0, blocking collectives: 26.2 us -> none  [on_device(): lax.psum((grad_gain_one, grad_gain_two), 'dp')]
    add x0 -> x20, other arithmetic: none -> 25.9 us  [the longest x14 23.9 us: permute_sum(): mine + theirs.astype(jnp.float32)]
  transfers between devices with their start and end apart: 6 -> 53, of which waited for: 6 -> 28; matrix products, arithmetic and copies ran while one was open for 6% -> 27% of each run, Pallas kernels for 0% -> 0%
where the time goes in v2:
time: 924 us; the launch traced here: 920 us
  waiting for transfers between devices  494 us (53%)
  matrix products  174 us (19%)
  other arithmetic  148 us (16%)
  starting transfers between devices  42.3 us (5%)
  local copies, waits for them, and re-layouts  35.2 us (4%)
  between operations  15.7 us (2%)
  blocking collectives  10.9 us (1%)
    ppermute x21, waiting for transfers between devices, permute_sum(): got = lax.ppermute(pieces, axis, partner_perm(size, 1 << step))  123 us
    ppermute x21, waiting for transfers between devices, permute_sum(): got = lax.ppermute(send, axis, partner_perm(size, 1 << step))  117 us
    psum x1, waiting for transfers between devices, on_device(): lax.psum(jnp.dot(attended, w_out, preferred_element_type=jnp.float32).ast...  86.2 us
    psum x1, waiting for transfers between devices, on_device(): lax.psum(jnp.dot(hidden, w_down, preferred_element_type=jnp.float32).asty...  82.8 us
    dot_general x15, matrix products, right_trans(): lax.dot_general(left, right, (((1,), (1,)), ((), ())), preferred_element_...  72.6 us
    psum x1, waiting for transfers between devices, on_device(): lax.psum((right_trans(d_gate, w_gate) + right_trans(d_up, w_up)).astype(j...  55.2 us
    dot_general x15, matrix products, left_trans(): lax.dot_general(left, right, (((0,), (0,)), ((), ())), preferred_element_...  45.3 us
    convert_element_type x2, other arithmetic, on_device(): d_scores = (probs * (d_probs - row_delta)).astype(jnp.bfloat16)  28.1 us
  transfers between devices with their start and end apart: 53, of which 28 were waited for; matrix products, arithmetic and copies ran while one was open for 27% of the time, Pallas kernels for 0%

profile of v2, /device:TPU:0, one launch (start us, length us, event | category | flops | bytes accessed | tf_op | source)
XLA Modules:
  0.0 919.7 jit_solution(16879764175254552638)
XLA Ops:
  19.7 10.9 %all-gather = bf16[8,1,512]{2,1,0:T(2,128)(2,1)S(1)} all-gather(bf16[1,1,512]{2,1,0:T(2,128)(2,1)S(1)} %reshape.237), channel_id=1, replica_groups=mesh['dp'=8,'tensor'=4] {'dp'}, dimensions={0}, use_global_device_ids=true | all-gather | bytes 9216 | tf_op jit(solution)/shard_map/all_gather | solution.py:162
  30.7 3.7 fusion.102
  34.7 25.2 %all-gather.3.cloned.1.call-done = bf16[4096,512]{0,1:T(8,128)(2,1)} async-done(((bf16[512,512]{0,1:T(8,128)(2,1)}), bf16[4096,512]{0,1:T(8,128)(2,1)}) %all-gather.3.cloned.1.call-update) | async-done | bytes 4194320 | tf_op jit(solution)/shard_map/all_gather | solution.py:157
  59.9 4.7 fusion.110
  64.6 3.4 copy-done.10
  70.2 3.5 fusion.111
  75.0 3.7 fusion.112
  80.0 5.5 fusion.113
  86.8 7.1 fusion.38
  103.0 86.2 %all-reduce.5.cloned.1.call-done = bf16[512,2048]{1,0:T(8,128)(2,1)} async-done(((bf16[512,2048]{1,0:T(8,128)(2,1)}), bf16[512,2048]{1,0:T(8,128)(2,1)}) %all-reduce.5.cloned.1.call-update) | async-done | bytes 2097168 | tf_op jit(solution)/shard_map/psum | solution.py:177
  189.2 3.3 multiply_reduce_fusion.4
  193.7 8.9 fusion.115
  202.5 5.0 fusion.114
  207.5 7.5 multiply_convert_fusion.6
  215.0 3.4 fusion.116
  218.5 6.3 fusion.119
  224.8 4.6 add_convert_fusion.1
  229.7 5.4 fusion.42
  237.5 7.1 dynamic-slice_convert_fusion.1
  245.1 3.5 fusion.118
  248.6 4.4 copy-done.37
  254.9 4.6 convolution_convert_fusion.1
  259.5 55.2 %all-reduce.7.cloned.1.call-done = bf16[512,2048]{1,0:T(8,128)(2,1)} async-done(((bf16[512,2048]{1,0:T(8,128)(2,1)}), bf16[512,2048]{1,0:T(8,128)(2,1)}) %all-reduce.7.cloned.1.call-update) | async-done | bytes 2097168 | tf_op jit(solution)/shard_map/psum | solution.py:200
  314.8 4.9 fusion.19
  319.7 3.5 convert_add_fusion.4
  327.1 4.9 fusion.28
  332.0 3.6 fusion.25
  336.8 6.6 fusion.12
  343.4 4.6 fusion.13
  348.0 4.6 fusion.46
  352.6 4.5 fusion.48
  357.1 4.6 fusion.58
  361.8 20.2 %multiply_reduce_fusion.2 = (f32[512]{0:T(512)S(1)}, f32[512]{0:T(512)S(1)}, f32[512]{0:T(512)S(1)}, f32[512]{0:T(512)S(1)}, f32[512,4096]{1,0:T(8,128)}) fusion(f32[512,4096]{1,0:T(8,128)S(1)} %bitcast.53, f32[512]{0:T(512)S(1)} %get-tuple-element.97, s32[512]{0:T(512)S(1)} %copy-done.74, pred[4096]{0:T(1024)(128)(4,1)S(1)} %bitcast.95, ...), kind=kOutput, calls=%fused_computation.7 | convolution fusion | flops 578811904 | bytes 68329472 | tf_op jit(solution)/shard_map/dot_general | solution.py:44
  381.9 10.0 %multiply_convert_fusion = bf16[512,4096]{1,0:T(8,128)(2,1)} fusion(f32[512,4096]{1,0:T(8,128)} %fusion.46, f32[512]{0:T(512)S(1)} %get-tuple-element.18, f32[512,4096]{1,0:T(8,128)} %copy-done.10, f32[512]{0:T(512)S(1)} %get-tuple-element.95, s32[512]{0:T(512)S(1)} %copy-done.74, pred[4096]{0:T(1024)(128)(4,1)S(1)} %bitcast.96, s32[512]{0:T(512)S(1)} %copy-done.72, ...), kind=kLoop, calls=%fused_computation | loop fusion | flops 18874368 | bytes 21000192 | tf_op jit(solution)/shard_map/convert_element_type | solution.py:228
  391.9 18.2 %multiply_convert_fusion.2 = (bf16[512,4096]{1,0:T(8,128)(2,1)}, bf16[512,4096]{1,0:T(8,128)(2,1)}, bf16[512,4096]{1,0:T(8,128)(2,1)}) fusion(f32[512,4096]{1,0:T(8,128)} %get-tuple-element.94, f32[512]{0:T(512)S(1)} %get-tuple-element.15, f32[512,4096]{1,0:T(8,128)S(1)} %bitcast.53, f32[512]{0:T(512)S(1)} %get-tuple-element.97, s32[512]{0:T(512)S(1)} %copy-done.74, ...), kind=kLoop, calls=%fused_computation.6 | loop fusion | flops 39845888 | bytes 62951424 | tf_op jit(solution)/shard_map/convert_element_type | solution.py:228
  420.9 4.2 convolution_multiply_fusion.2
  443.3 5.0 convert_add_fusion.1
  451.2 4.2 convert_add_fusion.2
  462.2 4.0 convert_add_fusion.3
  466.2 68.0 %collective-permute-done.22 = bf16[512,512]{1,0:T(8,128)(2,1)} collective-permute-done((bf16[512,512]{1,0:T(8,128)(2,1)}, bf16[512,512]{1,0:T(8,128)(2,1)}, u32[]{:S(2)}, u32[]{:S(2)}) %collective-permute-start.22) | collective-permute-done | bytes 524320 | tf_op jit(solution)/shard_map/ppermute | solution.py:68
  537.0 8.2 collective-permute-done.4
  548.3 6.4 collective-permute-done.5
  556.3 4.0 collective-permute-done.24
  560.8 4.1 collective-permute-done.6
  571.7 10.6 %collective-permute-done.31 = bf16[512,1408]{1,0:T(8,128)(2,1)S(1)} collective-permute-done((bf16[512,1408]{1,0:T(8,128)(2,1)S(1)}, bf16[512,1408]{1,0:T(8,128)(2,1)S(1)}, u32[]{:S(2)}, u32[]{:S(2)}) %collective-permute-start.31) | collective-permute-done | bytes 1441824 | tf_op jit(solution)/shard_map/ppermute | solution.py:68
  584.3 9.3 %collective-permute-done.25 = bf16[512,512]{1,0:T(8,128)(2,1)S(1)} collective-permute-done((bf16[512,512]{1,0:T(8,128)(2,1)S(1)}, bf16[512,512]{1,0:T(8,128)(2,1)S(1)}, u32[]{:S(2)}, u32[]{:S(2)}) %collective-permute-start.25) | collective-permute-done | bytes 524320 | tf_op jit(solution)/shard_map/ppermute | solution.py:73
  594.0 9.3 %collective-permute-done.7 = bf16[512,512]{1,0:T(8,128)(2,1)S(1)} collective-permute-done((bf16[512,512]{1,0:T(8,128)(2,1)S(1)}, bf16[512,512]{1,0:T(8,128)(2,1)S(1)}, u32[]{:S(2)}, u32[]{:S(2)}) %collective-permute-start.7) | collective-permute-done | bytes 524320 | tf_op jit(solution)/shard_map/ppermute | solution.py:73
  606.3 11.1 %collective-permute-done.32 = bf16[256,1408]{1,0:T(8,128)(2,1)S(1)} collective-permute-done((bf16[256,1408]{1,0:T(8,128)(2,1)S(1)}, bf16[256,1408]{1,0:T(8,128)(2,1)S(1)}, u32[]{:S(2)}, u32[]{:S(2)}) %collective-permute-start.32) | collective-permute-done | bytes 720928 | tf_op jit(solution)/shard_map/ppermute | solution.py:68
  619.3 13.5 %collective-permute-done.45 = bf16[1408,256]{1,0:T(8,128)(2,1)S(1)} collective-permute-done((bf16[1408,256]{1,0:T(8,128)(2,1)S(1)}, bf16[1408,256]{1,0:T(8,128)(2,1)S(1)}, u32[]{:S(2)}, u32[]{:S(2)}) %collective-permute-start.45) | collective-permute-done | bytes 720928 | tf_op jit(solution)/shard_map/ppermute | solution.py:73
  634.8 13.5 %collective-permute-done.39 = bf16[256,1408]{1,0:T(8,128)(2,1)S(1)} collective-permute-done((bf16[256,1408]{1,0:T(8,128)(2,1)S(1)}, bf16[256,1408]{1,0:T(8,128)(2,1)S(1)}, u32[]{:S(2)}, u32[]{:S(2)}) %collective-permute-start.39) | collective-permute-done | bytes 720928 | tf_op jit(solution)/shard_map/ppermute | solution.py:73
  650.3 11.3 %collective-permute-done.33 = bf16[256,1408]{1,0:T(8,128)(2,1)S(1)} collective-permute-done((bf16[256,1408]{1,0:T(8,128)(2,1)S(1)}, bf16[256,1408]{1,0:T(8,128)(2,1)S(1)}, u32[]{:S(2)}, u32[]{:S(2)}) %collective-permute-start.33) | collective-permute-done | bytes 720928 | tf_op jit(solution)/shard_map/ppermute | solution.py:73
  672.4 26.1 %collective-permute-done.40 = bf16[512,1408]{1,0:T(8,128)(2,1)S(1)} collective-permute-done((bf16[512,1408]{1,0:T(8,128)(2,1)S(1)}, bf16[512,1408]{1,0:T(8,128)(2,1)S(1)}, u32[]{:S(2)}, u32[]{:S(2)}) %collective-permute-start.40) | collective-permute-done | bytes 1441824 | tf_op jit(solution)/shard_map/ppermute | solution.py:73
  701.0 23.3 %collective-permute-done.34 = bf16[512,1408]{1,0:T(8,128)(2,1)S(1)} collective-permute-done((bf16[512,1408]{1,0:T(8,128)(2,1)S(1)}, bf16[512,1408]{1,0:T(8,128)(2,1)S(1)}, u32[]{:S(2)}, u32[]{:S(2)}) %collective-permute-start.34) | collective-permute-done | bytes 1441824 | tf_op jit(solution)/shard_map/ppermute | solution.py:73
  745.1 5.5 collective-permute-done.10
  757.7 4.1 collective-permute-done.17
  768.5 4.6 collective-permute-done.13
  779.9 5.6 broadcast_select_fusion.3
  785.5 6.9 broadcast_select_fusion.5
  792.4 5.9 maximum_convert_fusion.2
  798.3 5.7 maximum_convert_fusion.1
  804.0 5.2 maximum_convert_fusion
  813.3 82.8 %all-reduce.9.cloned.1.call-done = (bf16[512,2048]{1,0:T(8,128)(2,1)}, bf16[512,2048]{1,0:T(8,128)(2,1)}) async-done(((bf16[512,2048]{1,0:T(8,128)(2,1)}, bf16[512,2048]{1,0:T(8,128)(2,1)}), (bf16[512,2048]{1,0:T(8,128)(2,1)}, bf16[512,2048]{1,0:T(8,128)(2,1)})) %all-reduce.9.cloned.1.call-update) | async-done | bytes 4194320 | tf_op jit(solution)/shard_map/psum | solution.py:187
  896.1 3.5 fusion.20
  906.3 6.2 fusion.21
  (432 shorter events, 168.7 us)
Async XLA Ops:
  7.2 93.1 %copy-start = (bf16[512,2048]{1,0:T(8,128)(2,1)S(1)}, bf16[512,2048]{1,0:T(8,128)(2,1)}, u32[]{:S(2)}) copy-start(bf16[512,2048]{1,0:T(8,128)(2,1)} %param.20) | copy-start | bytes 6291460
  7.2 52.7 %all-gather.3.cloned.1.call-start = ((), (), s32[]{:S(2)}) async-start(), calls=%async_computation.1 | async-start | bytes 4718592 | tf_op jit(solution)/shard_map/all_gather | solution.py:157
  11.8 68.2 %copy-start.63 = (s32[2,2,8,128]{3,1,2,0:T(2,128)}, s32[2,2,8,128]{3,1,2,0:T(2,128)S(1)}, u32[]{:S(2)}) copy-start(s32[2,2,8,128]{3,1,2,0:T(2,128)S(1)} %copy.24) | copy-start | bytes 49156
  16.4 63.6 %copy-start.71 = (s32[512]{0:T(512)}, s32[512]{0:T(512)S(1)}, u32[]{:S(2)}) copy-start(s32[512]{0:T(512)S(1)} %get-tuple-element.22) | copy-start | bytes 6148
  19.6 169.5 %all-reduce.5.cloned.1.call-start = ((), (), s32[]{:S(2)}) async-start(), calls=%async_computation.2 | async-start | bytes 4194304 | tf_op jit(solution)/shard_map/psum | solution.py:177
  19.7 304.9 %copy-start.65 = (f32[512]{0:T(512)}, f32[512]{0:T(512)S(1)}, u32[]{:S(2)}) copy-start(f32[512]{0:T(512)S(1)} %get-tuple-element.84) | copy-start | bytes 6148
  30.7 49.3 %copy-start.67 = (pred[1,4,8,128]{3,1,2,0:T(4,128)(4,1)}, pred[1,4,8,128]{3,1,2,0:T(4,128)(4,1)S(1)}, u32[]{:S(2)}) copy-start(pred[1,4,8,128]{3,1,2,0:T(4,128)(4,1)S(1)} %copy.25) | copy-start | bytes 12292
  30.7 49.3 %copy-start.73 = (s32[512]{0:T(512)}, s32[512]{0:T(512)S(1)}, u32[]{:S(2)}) copy-start(s32[512]{0:T(512)S(1)} %iota_add_fusion) | copy-start | bytes 6148
  34.7 45.3 %copy-start.46 = (bf16[512,4,128]{0,2,1:T(8,128)(2,1)}, bf16[512,4,128]{0,2,1:T(8,128)(2,1)S(1)}, u32[]{:S(2)}) copy-start(bf16[512,4,128]{0,2,1:T(8,128)(2,1)S(1)} %pad_maximum_fusion.10) | copy-start | bytes 1572868
  102.9 211.9 %all-reduce.7.cloned.1.call-start = ((), (), s32[]{:S(2)}) async-start(), calls=%async_computation.3 | async-start | bytes 4194304 | tf_op jit(solution)/shard_map/psum | solution.py:200
  229.5 498.4 %reduce-scatter.2.cloned.1.call-start = ((), (), s32[]{:S(2)}) async-start(), calls=%async_computation.4 | async-start | bytes 4718592 | tf_op jit(solution)/shard_map/reduce_scatter | solution.py:238
  237.5 205.8 %collective-permute-start.42 = (bf16[1408,1024]{1,0:T(8,128)(2,1)}, bf16[1408,1024]{1,0:T(8,128)(2,1)}, u32[]{:S(2)}, u32[]{:S(2)}) collective-permute-start(bf16[1408,1024]{1,0:T(8,128)(2,1)} %dynamic-slice_convert_fusion), channel_id=1, source_target_pairs={{0,4},{4,0},{8,12},{12,8},{16,20},{20,16},{24,28},{28,24},{1,5},{5... | collective-permute-start | bytes 8650760 | tf_op jit(solution)/shard_map/ppermute | solution.py:68
  244.6 206.6 %collective-permute-start.36 = (bf16[1024,1408]{1,0:T(8,128)(2,1)}, bf16[1024,1408]{1,0:T(8,128)(2,1)}, u32[]{:S(2)}, u32[]{:S(2)}) collective-permute-start(bf16[1024,1408]{1,0:T(8,128)(2,1)} %dynamic-slice_convert_fusion.1), channel_id=1, source_target_pairs={{0,4},{4,0},{8,12},{12,8},{16,20},{20,16},{24,28},{28,24},{1,5},{5... | collective-permute-start | bytes 8650760 | tf_op jit(solution)/shard_map/ppermute | solution.py:68
  254.9 207.3 %collective-permute-start.30 = (bf16[1024,1408]{1,0:T(8,128)(2,1)}, bf16[1024,1408]{1,0:T(8,128)(2,1)}, u32[]{:S(2)}, u32[]{:S(2)}) collective-permute-start(bf16[1024,1408]{1,0:T(8,128)(2,1)} %dynamic-slice_convert_fusion.2), channel_id=1, source_target_pairs={{0,4},{4,0},{8,12},{12,8},{16,20},{20,16},{24,28},{28,24},{1,5},{5... | collective-permute-start | bytes 8650760 | tf_op jit(solution)/shard_map/ppermute | solution.py:68
  326.0 108.6 %collective-permute-start.27 = (f32[2048]{0:T(1024)S(1)}, f32[2048]{0:T(1024)}, u32[]{:S(2)}, u32[]{:S(2)}) collective-permute-start(f32[2048]{0:T(1024)S(1)} %get-tuple-element.11), channel_id=1, source_target_pairs={{0,4},{4,0},{8,12},{12,8},{16,20},{20,16},{24,28},{28,24},{1,5},{5... | collective-permute-start | bytes 24584 | tf_op jit(solution)/shard_map/ppermute | solution.py:87
  336.8 120.4 %collective-permute-start.21 = (bf16[512,1024]{1,0:T(8,128)(2,1)}, bf16[512,1024]{1,0:T(8,128)(2,1)}, u32[]{:S(2)}, u32[]{:S(2)}) collective-permute-start(bf16[512,1024]{1,0:T(8,128)(2,1)} %dynamic-slice_convert_fusion.6), channel_id=1, source_target_pairs={{0,4},{4,0},{8,12},{12,8},{16,20},{20,16},{24,28},{28,24},{1,5},{5... | collective-permute-start | bytes 3145736 | tf_op jit(solution)/shard_map/ppermute | solution.py:68
  420.6 475.5 %all-reduce.9.cloned.1.call-start = ((), (), s32[]{:S(2)}) async-start(), calls=%async_computation.5 | async-start | bytes 8388608 | tf_op jit(solution)/shard_map/psum | solution.py:187
  435.4 3.7 collective-permute-start.28
  439.0 3.7 collective-permute-start.29
  442.7 18.6 %collective-permute-start.3 = (bf16[1024,512]{1,0:T(8,128)(2,1)S(1)}, bf16[1024,512]{1,0:T(8,128)(2,1)S(1)}, u32[]{:S(2)}, u32[]{:S(2)}) collective-permute-start(bf16[1024,512]{1,0:T(8,128)(2,1)S(1)} %dynamic-slice_convert_fusion.7), channel_id=1, source_target_pairs={{0,4},{4,0},{8,12},{12,8},{16,20},{20,16},{24,28},{28,24},{1,5},{5... | collective-permute-start | bytes 3145736 | tf_op jit(solution)/shard_map/ppermute | solution.py:68
  449.6 115.8 %collective-permute-start.43 = (bf16[1408,512]{1,0:T(8,128)(2,1)}, bf16[1408,512]{1,0:T(8,128)(2,1)}, u32[]{:S(2)}, u32[]{:S(2)}) collective-permute-start(bf16[1408,512]{1,0:T(8,128)(2,1)} %dynamic-slice_convert_fusion.3), channel_id=1, source_target_pairs={{0,8},{4,12},{8,0},{12,4},{16,24},{20,28},{24,16},{28,20},{1,9},{5... | collective-permute-start | bytes 4325384 | tf_op jit(solution)/shard_map/ppermute | solution.py:68
  456.7 112.5 %collective-permute-start.37 = (bf16[512,1408]{1,0:T(8,128)(2,1)}, bf16[512,1408]{1,0:T(8,128)(2,1)}, u32[]{:S(2)}, u32[]{:S(2)}) collective-permute-start(bf16[512,1408]{1,0:T(8,128)(2,1)} %dynamic-slice_convert_fusion.4), channel_id=1, source_target_pairs={{0,8},{4,12},{8,0},{12,4},{16,24},{20,28},{24,16},{28,20},{1,9},{5... | collective-permute-start | bytes 4325384 | tf_op jit(solution)/shard_map/ppermute | solution.py:68
  459.7 74.5 %collective-permute-start.22 = (bf16[512,512]{1,0:T(8,128)(2,1)}, bf16[512,512]{1,0:T(8,128)(2,1)}, u32[]{:S(2)}, u32[]{:S(2)}) collective-permute-start(bf16[512,512]{1,0:T(8,128)(2,1)} %dynamic-slice_convert_fusion.11), channel_id=1, source_target_pairs={{0,8},{4,12},{8,0},{12,4},{16,24},{20,28},{24,16},{28,20},{1,9},{5... | collective-permute-start | bytes 1572872 | tf_op jit(solution)/shard_map/ppermute | solution.py:68
  461.7 83.5 %collective-permute-start.4 = (bf16[512,512]{1,0:T(8,128)(2,1)S(1)}, bf16[512,512]{1,0:T(8,128)(2,1)S(1)}, u32[]{:S(2)}, u32[]{:S(2)}) collective-permute-start(bf16[512,512]{1,0:T(8,128)(2,1)S(1)} %dynamic-slice_convert_fusion.14), channel_id=1, source_target_pairs={{0,8},{4,12},{8,0},{12,4},{16,24},{20,28},{24,16},{28,20},{1,9},{5... | collective-permute-start | bytes 1572872 | tf_op jit(solution)/shard_map/ppermute | solution.py:68
  535.5 11.5 %collective-permute-start.23 = (bf16[512,256]{1,0:T(8,128)(2,1)S(1)}, bf16[512,256]{1,0:T(8,128)(2,1)S(1)}, u32[]{:S(2)}, u32[]{:S(2)}) collective-permute-start(bf16[512,256]{1,0:T(8,128)(2,1)S(1)} %dynamic-slice_convert_fusion.15), channel_id=1, source_target_pairs={{0,16},{4,20},{8,24},{12,28},{16,0},{20,4},{24,8},{28,12},{1,17},{... | collective-permute-start | bytes 786440 | tf_op jit(solution)/shard_map/ppermute | solution.py:68
  545.4 9.2 %collective-permute-start.5 = (bf16[256,512]{1,0:T(8,128)(2,1)S(1)}, bf16[256,512]{1,0:T(8,128)(2,1)S(1)}, u32[]{:S(2)}, u32[]{:S(2)}) collective-permute-start(bf16[256,512]{1,0:T(8,128)(2,1)S(1)} %dynamic-slice_convert_fusion.18), channel_id=1, source_target_pairs={{0,16},{4,20},{8,24},{12,28},{16,0},{20,4},{24,8},{28,12},{1,17},{... | collective-permute-start | bytes 786440 | tf_op jit(solution)/shard_map/ppermute | solution.py:68
  547.1 13.2 %collective-permute-start.24 = (bf16[512,256]{1,0:T(8,128)(2,1)S(1)}, bf16[512,256]{1,0:T(8,128)(2,1)S(1)}, u32[]{:S(2)}, u32[]{:S(2)}) collective-permute-start(bf16[512,256]{1,0:T(8,128)(2,1)S(1)} %add_convert_fusion.6), channel_id=1, source_target_pairs={{0,16},{4,20},{8,24},{12,28},{16,0},{20,4},{24,8},{28,12},{1,17},{... | collective-permute-start | bytes 786440 | tf_op jit(solution)/shard_map/ppermute | solution.py:73
  547.9 34.5 %collective-permute-start.31 = (bf16[512,1408]{1,0:T(8,128)(2,1)S(1)}, bf16[512,1408]{1,0:T(8,128)(2,1)S(1)}, u32[]{:S(2)}, u32[]{:S(2)}) collective-permute-start(bf16[512,1408]{1,0:T(8,128)(2,1)S(1)} %dynamic-slice_convert_fusion.5), channel_id=1, source_target_pairs={{0,8},{4,12},{8,0},{12,4},{16,24},{20,28},{24,16},{28,20},{1,9},{5... | collective-permute-start | bytes 4325384 | tf_op jit(solution)/shard_map/ppermute | solution.py:68
  554.8 10.2 %collective-permute-start.6 = (bf16[256,512]{1,0:T(8,128)(2,1)S(1)}, bf16[256,512]{1,0:T(8,128)(2,1)S(1)}, u32[]{:S(2)}, u32[]{:S(2)}) collective-permute-start(bf16[256,512]{1,0:T(8,128)(2,1)S(1)} %add_convert_fusion.7), channel_id=1, source_target_pairs={{0,16},{4,20},{8,24},{12,28},{16,0},{20,4},{24,8},{28,12},{1,17},{... | collective-permute-start | bytes 786440 | tf_op jit(solution)/shard_map/ppermute | solution.py:73
  560.4 33.2 %collective-permute-start.25 = (bf16[512,512]{1,0:T(8,128)(2,1)S(1)}, bf16[512,512]{1,0:T(8,128)(2,1)S(1)}, u32[]{:S(2)}, u32[]{:S(2)}) collective-permute-start(bf16[512,512]{1,0:T(8,128)(2,1)S(1)} %pad_maximum_fusion.17), channel_id=1, source_target_pairs={{0,8},{4,12},{8,0},{12,4},{16,24},{20,28},{24,16},{28,20},{1,9},{5... | collective-permute-start | bytes 1572872 | tf_op jit(solution)/shard_map/ppermute | solution.py:73
  565.0 38.3 %collective-permute-start.7 = (bf16[512,512]{1,0:T(8,128)(2,1)S(1)}, bf16[512,512]{1,0:T(8,128)(2,1)S(1)}, u32[]{:S(2)}, u32[]{:S(2)}) collective-permute-start(bf16[512,512]{1,0:T(8,128)(2,1)S(1)} %pad_maximum_fusion.14), channel_id=1, source_target_pairs={{0,8},{4,12},{8,0},{12,4},{16,24},{20,28},{24,16},{28,20},{1,9},{5... | collective-permute-start | bytes 1572872 | tf_op jit(solution)/shard_map/ppermute | solution.py:73
  567.4 36.3 %collective-permute-start.44 = (bf16[1408,256]{1,0:T(8,128)(2,1)S(1)}, bf16[1408,256]{1,0:T(8,128)(2,1)S(1)}, u32[]{:S(2)}, u32[]{:S(2)}) collective-permute-start(bf16[1408,256]{1,0:T(8,128)(2,1)S(1)} %dynamic-slice_convert_fusion.8), channel_id=1, source_target_pairs={{0,16},{4,20},{8,24},{12,28},{16,0},{20,4},{24,8},{28,12},{1,17},{... | collective-permute-start | bytes 2162696 | tf_op jit(solution)/shard_map/ppermute | solution.py:68
  571.4 34.2 %collective-permute-start.38 = (bf16[256,1408]{1,0:T(8,128)(2,1)S(1)}, bf16[256,1408]{1,0:T(8,128)(2,1)S(1)}, u32[]{:S(2)}, u32[]{:S(2)}) collective-permute-start(bf16[256,1408]{1,0:T(8,128)(2,1)S(1)} %dynamic-slice_convert_fusion.9), channel_id=1, source_target_pairs={{0,16},{4,20},{8,24},{12,28},{16,0},{20,4},{24,8},{28,12},{1,17},{... | collective-permute-start | bytes 2162696 | tf_op jit(solution)/shard_map/ppermute | solution.py:68
  582.8 34.6 %collective-permute-start.32 = (bf16[256,1408]{1,0:T(8,128)(2,1)S(1)}, bf16[256,1408]{1,0:T(8,128)(2,1)S(1)}, u32[]{:S(2)}, u32[]{:S(2)}) collective-permute-start(bf16[256,1408]{1,0:T(8,128)(2,1)S(1)} %dynamic-slice_convert_fusion.10), channel_id=1, source_target_pairs={{0,16},{4,20},{8,24},{12,28},{16,0},{20,4},{24,8},{28,12},{1,17},{... | collective-permute-start | bytes 2162696 | tf_op jit(solution)/shard_map/ppermute | solution.py:68
  593.9 69.7 %collective-permute-start.26 = (bf16[512,1024]{1,0:T(8,128)(2,1)S(1)}, bf16[512,1024]{1,0:T(8,128)(2,1)S(1)}, u32[]{:S(2)}, u32[]{:S(2)}) collective-permute-start(bf16[512,1024]{1,0:T(8,128)(2,1)S(1)} %pad_maximum_fusion.9), channel_id=1, source_target_pairs={{0,4},{4,0},{8,12},{12,8},{16,20},{20,16},{24,28},{28,24},{1,5},{5... | collective-permute-start | bytes 3145736 | tf_op jit(solution)/shard_map/ppermute | solution.py:73
  603.6 63.1 %collective-permute-start.8 = (bf16[1024,512]{1,0:T(8,128)(2,1)S(1)}, bf16[1024,512]{1,0:T(8,128)(2,1)S(1)}, u32[]{:S(2)}, u32[]{:S(2)}) collective-permute-start(bf16[1024,512]{1,0:T(8,128)(2,1)S(1)} %pad_maximum_fusion.8), channel_id=1, source_target_pairs={{0,4},{4,0},{8,12},{12,8},{16,20},{20,16},{24,28},{28,24},{1,5},{5... | collective-permute-start | bytes 3145736 | tf_op jit(solution)/shard_map/ppermute | solution.py:73
  604.0 28.8 %collective-permute-start.45 = (bf16[1408,256]{1,0:T(8,128)(2,1)S(1)}, bf16[1408,256]{1,0:T(8,128)(2,1)S(1)}, u32[]{:S(2)}, u32[]{:S(2)}) collective-permute-start(bf16[1408,256]{1,0:T(8,128)(2,1)S(1)} %add_convert_fusion.3), channel_id=1, source_target_pairs={{0,16},{4,20},{8,24},{12,28},{16,0},{20,4},{24,8},{28,12},{1,17},{... | collective-permute-start | bytes 2162696 | tf_op jit(solution)/shard_map/ppermute | solution.py:73
  605.7 42.6 %collective-permute-start.39 = (bf16[256,1408]{1,0:T(8,128)(2,1)S(1)}, bf16[256,1408]{1,0:T(8,128)(2,1)S(1)}, u32[]{:S(2)}, u32[]{:S(2)}) collective-permute-start(bf16[256,1408]{1,0:T(8,128)(2,1)S(1)} %add_convert_fusion.4), channel_id=1, source_target_pairs={{0,16},{4,20},{8,24},{12,28},{16,0},{20,4},{24,8},{28,12},{1,17},{... | collective-permute-start | bytes 2162696 | tf_op jit(solution)/shard_map/ppermute | solution.py:73
  617.5 44.1 %collective-permute-start.33 = (bf16[256,1408]{1,0:T(8,128)(2,1)S(1)}, bf16[256,1408]{1,0:T(8,128)(2,1)S(1)}, u32[]{:S(2)}, u32[]{:S(2)}) collective-permute-start(bf16[256,1408]{1,0:T(8,128)(2,1)S(1)} %add_convert_fusion.5), channel_id=1, source_target_pairs={{0,16},{4,20},{8,24},{12,28},{16,0},{20,4},{24,8},{28,12},{1,17},{... | collective-permute-start | bytes 2162696 | tf_op jit(solution)/shard_map/ppermute | solution.py:73
  633.1 36.7 %collective-permute-start.46 = (bf16[1408,512]{1,0:T(8,128)(2,1)S(1)}, bf16[1408,512]{1,0:T(8,128)(2,1)S(1)}, u32[]{:S(2)}, u32[]{:S(2)}) collective-permute-start(bf16[1408,512]{1,0:T(8,128)(2,1)S(1)} %pad_maximum_fusion.6), channel_id=1, source_target_pairs={{0,8},{4,12},{8,0},{12,4},{16,24},{20,28},{24,16},{28,20},{1,9},{5... | collective-permute-start | bytes 4325384 | tf_op jit(solution)/shard_map/ppermute | solution.py:73
  648.6 49.9 %collective-permute-start.40 = (bf16[512,1408]{1,0:T(8,128)(2,1)S(1)}, bf16[512,1408]{1,0:T(8,128)(2,1)S(1)}, u32[]{:S(2)}, u32[]{:S(2)}) collective-permute-start(bf16[512,1408]{1,0:T(8,128)(2,1)S(1)} %pad_maximum_fusion.5), channel_id=1, source_target_pairs={{0,8},{4,12},{8,0},{12,4},{16,24},{20,28},{24,16},{28,20},{1,9},{5... | collective-permute-start | bytes 4325384 | tf_op jit(solution)/shard_map/ppermute | solution.py:73
  661.9 62.4 %collective-permute-start.34 = (bf16[512,1408]{1,0:T(8,128)(2,1)S(1)}, bf16[512,1408]{1,0:T(8,128)(2,1)S(1)}, u32[]{:S(2)}, u32[]{:S(2)}) collective-permute-start(bf16[512,1408]{1,0:T(8,128)(2,1)S(1)} %pad_maximum_fusion.4), channel_id=1, source_target_pairs={{0,8},{4,12},{8,0},{12,4},{16,24},{20,28},{24,16},{28,20},{1,9},{5... | collective-permute-start | bytes 4325384 | tf_op jit(solution)/shard_map/ppermute | solution.py:73
  670.4 28.7 %copy-start.23 = (bf16[1408,512]{1,0:T(8,128)(2,1)}, bf16[1408,512]{1,0:T(8,128)(2,1)S(1)}, u32[]{:S(2)}) copy-start(bf16[1408,512]{1,0:T(8,128)(2,1)S(1)} %get-tuple-element.33) | copy-start | bytes 4325380
  672.4 104.5 %collective-permute-start.47 = (bf16[1408,1024]{1,0:T(8,128)(2,1)}, bf16[1408,1024]{1,0:T(8,128)(2,1)}, u32[]{:S(2)}, u32[]{:S(2)}) collective-permute-start(bf16[1408,1024]{1,0:T(8,128)(2,1)} %pad_maximum_fusion.3), channel_id=1, source_target_pairs={{0,4},{4,0},{8,12},{12,8},{16,20},{20,16},{24,28},{28,24},{1,5},{5... | collective-permute-start | bytes 8650760 | tf_op jit(solution)/shard_map/ppermute | solution.py:73
  701.0 78.8 %collective-permute-start.41 = (bf16[1024,1408]{1,0:T(8,128)(2,1)}, bf16[1024,1408]{1,0:T(8,128)(2,1)}, u32[]{:S(2)}, u32[]{:S(2)}) collective-permute-start(bf16[1024,1408]{1,0:T(8,128)(2,1)} %pad_maximum_fusion.2), channel_id=1, source_target_pairs={{0,4},{4,0},{8,12},{12,8},{16,20},{20,16},{24,28},{28,24},{1,5},{5... | collective-permute-start | bytes 8650760 | tf_op jit(solution)/shard_map/ppermute | solution.py:73
  727.8 57.6 %collective-permute-start.35 = (bf16[1024,1408]{1,0:T(8,128)(2,1)}, bf16[1024,1408]{1,0:T(8,128)(2,1)}, u32[]{:S(2)}, u32[]{:S(2)}) collective-permute-start(bf16[1024,1408]{1,0:T(8,128)(2,1)} %pad_maximum_fusion.1), channel_id=1, source_target_pairs={{0,4},{4,0},{8,12},{12,8},{16,20},{20,16},{24,28},{28,24},{1,5},{5... | collective-permute-start | bytes 8650760 | tf_op jit(solution)/shard_map/ppermute | solution.py:73
  732.8 7.0 collective-permute-start.9
  735.8 7.4 collective-permute-start.15
  741.4 9.2 %collective-permute-start.10 = (bf16[512,256]{1,0:T(8,128)(2,1)S(1)}, bf16[512,256]{1,0:T(8,128)(2,1)S(1)}, u32[]{:S(2)}, u32[]{:S(2)}) collective-permute-start(bf16[512,256]{1,0:T(8,128)(2,1)S(1)} %dynamic-slice_convert_fusion.17), channel_id=1, source_target_pairs={{0,8},{4,12},{8,0},{12,4},{16,24},{20,28},{24,16},{28,20},{1,9},{5... | collective-permute-start | bytes 786440 | tf_op jit(solution)/shard_map/ppermute | solution.py:68
  744.7 10.7 %collective-permute-start.16 = (bf16[512,256]{1,0:T(8,128)(2,1)S(1)}, bf16[512,256]{1,0:T(8,128)(2,1)S(1)}, u32[]{:S(2)}, u32[]{:S(2)}) collective-permute-start(bf16[512,256]{1,0:T(8,128)(2,1)S(1)} %dynamic-slice_convert_fusion.16), channel_id=1, source_target_pairs={{0,8},{4,12},{8,0},{12,4},{16,24},{20,28},{24,16},{28,20},{1,9},{5... | collective-permute-start | bytes 786440 | tf_op jit(solution)/shard_map/ppermute | solution.py:68
  750.8 26.1 %copy-start.24 = (bf16[1408,512]{1,0:T(8,128)(2,1)S(1)}, bf16[1408,512]{1,0:T(8,128)(2,1)}, u32[]{:S(2)}) copy-start(bf16[1408,512]{1,0:T(8,128)(2,1)} %copy-done.23) | copy-start | bytes 4325380
  750.8 6.5 collective-permute-start.11
  755.5 6.3 collective-permute-start.17
  757.3 7.3 collective-permute-start.12
  761.9 5.0 collective-permute-start.18
  764.7 8.5 collective-permute-start.13
  766.9 9.0 collective-permute-start.19
  774.1 35.1 %collective-permute-start.14 = (bf16[1024,256]{1,0:T(8,128)(2,1)}, bf16[1024,256]{1,0:T(8,128)(2,1)}, u32[]{:S(2)}, u32[]{:S(2)}) collective-permute-start(bf16[1024,256]{1,0:T(8,128)(2,1)} %pad_maximum_fusion.15), channel_id=1, source_target_pairs={{0,4},{4,0},{8,12},{12,8},{16,20},{20,16},{24,28},{28,24},{1,5},{5... | collective-permute-start | bytes 1572872 | tf_op jit(solution)/shard_map/ppermute | solution.py:73
  776.9 33.6 %collective-permute-start.20 = (bf16[1024,256]{1,0:T(8,128)(2,1)}, bf16[1024,256]{1,0:T(8,128)(2,1)}, u32[]{:S(2)}, u32[]{:S(2)}) collective-permute-start(bf16[1024,256]{1,0:T(8,128)(2,1)} %pad_maximum_fusion.16), channel_id=1, source_target_pairs={{0,4},{4,0},{8,12},{12,8},{16,20},{20,16},{24,28},{28,24},{1,5},{5... | collective-permute-start | bytes 1572872 | tf_op jit(solution)/shard_map/ppermute | solution.py:73
  813.3 89.3 %copy-start.76 = (f32[512]{0:T(512)S(1)}, f32[512]{0:T(512)}, u32[]{:S(2)}) copy-start(f32[512]{0:T(512)} %copy-done.75) | copy-start | bytes 6148
  813.3 93.0 %copy-start.66 = (f32[512]{0:T(512)S(1)}, f32[512]{0:T(512)}, u32[]{:S(2)}) copy-start(f32[512]{0:T(512)} %copy-done.65) | copy-start | bytes 6148
  899.5 1.6 collective-permute-start
  901.1 3.7 collective-permute-start.1
  904.8 7.7 collective-permute-start.2
  (87 other events, 619.4 us)
Sparse Core Ops, SparseCore 0:
  19.8 40.0 all-gather.2
  103.0 86.1 all-reduce.4
  229.6 85.1 all-reduce.6
  420.7 59.7 reduce-scatter.1
  740.0 156.0 all-reduce.8

commit v3 on v2

--- a/solution.py
+++ b/solution.py
@@ -174,9 +174,9 @@
         value_part = all_values[:, group_index * HEAD_DIM : (group_index + 1) * HEAD_DIM]
         mixed_parts.append(jnp.dot(probs_low, value_part, preferred_element_type=jnp.float32))
     attended = jnp.concatenate(mixed_parts, axis=1).astype(jnp.bfloat16)
-    branch = lax.psum(
-        jnp.dot(attended, w_out, preferred_element_type=jnp.float32).astype(jnp.bfloat16), "tensor"
-    ).astype(jnp.float32)
+    (branch,) = permute_sum(
+        [jnp.dot(attended, w_out, preferred_element_type=jnp.float32)], [0], "tensor"
+    )
     middle = source + keep_rows * branch
     normed_two_full, norm_two_back = jax.vjp(rms_norm, middle, gain_two.astype(jnp.float32))
     normed_two = normed_two_full.astype(jnp.bfloat16)
@@ -184,9 +184,9 @@
     up_value = jnp.dot(normed_two, w_up, preferred_element_type=jnp.float32)
     hidden_full, swiglu_back = jax.vjp(swiglu, gate_value, up_value)
     hidden = hidden_full.astype(jnp.bfloat16)
-    down_sum = lax.psum(
-        jnp.dot(hidden, w_down, preferred_element_type=jnp.float32).astype(jnp.bfloat16), "tensor"
-    ).astype(jnp.float32)
+    (down_sum,) = permute_sum(
+        [jnp.dot(hidden, w_down, preferred_element_type=jnp.float32)], [0], "tensor"
+    )
     output = (middle + keep_rows * down_sum).astype(jnp.bfloat16)
     grad_out = cotangent.astype(jnp.float32)
     d_down = (keep_rows * grad_out).astype(jnp.bfloat16)
@@ -197,9 +197,9 @@
     d_up = d_up_full.astype(jnp.bfloat16)
     grad_w_gate = left_trans(normed_two, d_gate)
     grad_w_up = left_trans(normed_two, d_up)
-    d_normed_two = lax.psum(
-        (right_trans(d_gate, w_gate) + right_trans(d_up, w_up)).astype(jnp.bfloat16), "tensor"
-    ).astype(jnp.float32)
+    (d_normed_two,) = permute_sum(
+        [right_trans(d_gate, w_gate) + right_trans(d_up, w_up)], [0], "tensor"
+    )
     d_middle_norm, grad_gain_two = norm_two_back(d_normed_two)
     grad_middle = grad_out + d_middle_norm
     d_branch = (keep_rows * grad_middle).astype(jnp.bfloat16)
@@ -263,18 +263,23 @@
         + right_trans(d_key_low, w_key)
         + right_trans(d_value_low, w_value)
     )
-    d_normed = lax.psum(d_normed_part.astype(jnp.bfloat16), "tensor").astype(jnp.float32)
+    (d_normed,) = permute_sum([d_normed_part], [0], "tensor")
     d_source_norm, grad_gain_one = norm_one_back(d_normed)
     grad_input = grad_middle + d_source_norm
     grad_gain_one = permute_allsum(grad_gain_one, "dp")
     grad_gain_two = permute_allsum(grad_gain_two, "dp")
-    grad_w_gate, grad_w_up, grad_w_down = permute_sum(
-        [grad_w_gate, grad_w_up, grad_w_down], [0, 0, 1], "dp"
-    )
-    (grad_w_out,) = permute_sum([grad_w_out], [1], "dp")
-    grad_w_query, grad_w_key, grad_w_value = permute_sum(
-        [grad_w_query, grad_w_key, grad_w_value], [0, 0, 0], "dp"
-    )
+    def dp_sum(grads):
+        return [lax.psum(grad.astype(jnp.bfloat16), "dp").astype(jnp.float32) for grad in grads]
+
+    grad_w_gate, grad_w_up, grad_w_down = dp_sum([grad_w_gate, grad_w_up, grad_w_down])
+    grad_w_gate, grad_w_up, grad_w_down, grad_w_out = lax.optimization_barrier(
+        (grad_w_gate, grad_w_up, grad_w_down, grad_w_out)
+    )
+    (grad_w_out,) = dp_sum([grad_w_out])
+    grad_w_out, grad_w_query, grad_w_key, grad_w_value = lax.optimization_barrier(
+        (grad_w_out, grad_w_query, grad_w_key, grad_w_value)
+    )
+    grad_w_query, grad_w_key, grad_w_value = dp_sum([grad_w_query, grad_w_key, grad_w_value])
     return (
         output,
         grad_input,

time: 924 us -> 971 us (1.051)
  waiting for transfers between devices: 494 us -> 623 us
  other arithmetic: 148 us -> 105 us
  starting transfers between devices: 42.3 us -> 23.5 us
  local copies, waits for them, and re-layouts: 35.2 us -> 17.8 us
    psum x3, waiting for transfers between devices: 224 us -> 292 us  [dp_sum(): lax.psum(grad.astype(jnp.bfloat16), 'dp').astype(jnp.float32)]
    ppermute x21 -> x8, waiting for transfers between devices: 117 us -> 151 us  [permute_sum(): got = lax.ppermute(send, axis, partner_perm(size, 1 << step))]
    add x14 -> x4, other arithmetic: 23.9 us -> 3.13 us  [permute_sum(): mine + theirs.astype(jnp.float32)]
    reduce_scatter x1, waiting for transfers between devices: 0.01 us -> 17.6 us  [on_device(): lax.psum_scatter(jnp.concatenate([d_key_all, d_value_all], axis=1).astype...]
    convert_element_type x21 -> x8, local copies, waits for them, and re-layouts: 18.6 us -> 1.62 us  [permute_sum(): lax.dynamic_slice_in_dim(piece, (1 - bit) * half, half, axis=dim)]
    select_n x21 -> x8, other arithmetic: 21.8 us -> 5.83 us  [permute_sum(): jnp.where(first, mine, theirs)]
    ppermute x21 -> x8, starting transfers between devices: 17.4 us -> 4.79 us  [permute_sum(): got = lax.ppermute(pieces, axis, partner_perm(size, 1 << step))]
    ppermute x21 -> x8, waiting for transfers between devices: 123 us -> 131 us  [permute_sum(): got = lax.ppermute(pieces, axis, partner_perm(size, 1 << step))]
  transfers between devices with their start and end apart: 53 -> 27, of which waited for: 28 -> 21; matrix products, arithmetic and copies ran while one was open for 27% -> 11% of each run, Pallas kernels for 0% -> 0%
where the time goes in v3:
time: 971 us; the launch traced here: 967 us
  waiting for transfers between devices  623 us (64%)
  matrix products  171 us (18%)
  other arithmetic  105 us (11%)
  starting transfers between devices  23.5 us (2%)
  local copies, waits for them, and re-layouts  17.8 us (2%)
  between operations  15.7 us (2%)
  blocking collectives  10.6 us (1%)
    psum x3, waiting for transfers between devices, dp_sum(): lax.psum(grad.astype(jnp.bfloat16), 'dp').astype(jnp.float32)  292 us
    ppermute x8, waiting for transfers between devices, permute_sum(): got = lax.ppermute(send, axis, partner_perm(size, 1 << step))  151 us
    ppermute x8, waiting for transfers between devices, permute_sum(): got = lax.ppermute(pieces, axis, partner_perm(size, 1 << step))  131 us
    dot_general x15, matrix products, right_trans(): lax.dot_general(left, right, (((1,), (1,)), ((), ())), preferred_element_...  71.3 us
    dot_general x15, matrix products, left_trans(): lax.dot_general(left, right, (((0,), (0,)), ((), ())), preferred_element_...  48.7 us
    convert_element_type x7, other arithmetic, dp_sum(): lax.psum(grad.astype(jnp.bfloat16), 'dp').astype(jnp.float32)  31.4 us
    convert_element_type x2, other arithmetic, on_device(): d_scores = (probs * (d_probs - row_delta)).astype(jnp.bfloat16)  27 us
    all_gather x1, waiting for transfers between devices, on_device(): lax.all_gather(jnp.concatenate([key_low, value_low], axis=1), 'dp', axis=...  25.4 us
  transfers between devices with their start and end apart: 27, of which 21 were waited for; matrix products, arithmetic and copies ran while one was open for 11% of the time, Pallas kernels for 0%

profile of v3, /device:TPU:0, one launch (start us, length us, event | category | flops | bytes accessed | tf_op | source)
XLA Modules:
  0.0 967.1 jit_solution(9074915309664158548)
XLA Ops:
  10.4 2.8 convolution_convert_fusion.4
  18.5 10.6 %all-gather = bf16[8,1,512]{2,1,0:T(2,128)(2,1)S(1)} all-gather(bf16[1,1,512]{2,1,0:T(2,128)(2,1)S(1)} %reshape.237), channel_id=1, replica_groups=mesh['dp'=8,'tensor'=4] {'dp'}, dimensions={0}, use_global_device_ids=true | all-gather | bytes 9216 | tf_op jit(solution)/shard_map/all_gather | solution.py:162
  29.2 3.7 fusion.102
  33.2 25.4 %all-gather.3.cloned.1.call-done = bf16[4096,512]{0,1:T(8,128)(2,1)} async-done(((bf16[512,512]{0,1:T(8,128)(2,1)}), bf16[4096,512]{0,1:T(8,128)(2,1)}) %all-gather.3.cloned.1.call-update) | async-done | bytes 4194320 | tf_op jit(solution)/shard_map/all_gather | solution.py:157
  58.6 4.7 fusion.110
  63.4 3.4 copy-done.9
  69.0 3.5 fusion.111
  73.8 3.9 fusion.112
  79.0 5.5 fusion.113
  85.9 7.1 fusion.38
  104.1 23.9 %collective-permute-done = bf16[256,2048]{1,0:T(8,128)(2,1)} collective-permute-done((bf16[256,2048]{1,0:T(8,128)(2,1)S(1)}, bf16[256,2048]{1,0:T(8,128)(2,1)}, u32[]{:S(2)}, u32[]{:S(2)}) %collective-permute-start) | collective-permute-done | bytes 1048608 | tf_op jit(solution)/shard_map/ppermute | solution.py:68
  134.1 23.0 %collective-permute-done.1 = bf16[128,2048]{1,0:T(8,128)(2,1)S(1)} collective-permute-done((bf16[128,2048]{1,0:T(8,128)(2,1)S(1)}, bf16[128,2048]{1,0:T(8,128)(2,1)S(1)}, u32[]{:S(2)}, u32[]{:S(2)}) %collective-permute-start.1) | collective-permute-done | bytes 524320 | tf_op jit(solution)/shard_map/ppermute | solution.py:68
  159.2 24.4 %collective-permute-done.2 = bf16[128,2048]{1,0:T(8,128)(2,1)} collective-permute-done((bf16[128,2048]{1,0:T(8,128)(2,1)S(1)}, bf16[128,2048]{1,0:T(8,128)(2,1)}, u32[]{:S(2)}, u32[]{:S(2)}) %collective-permute-start.2) | collective-permute-done | bytes 524320 | tf_op jit(solution)/shard_map/ppermute | solution.py:73
  186.0 6.5 fusion.43
  192.5 17.3 %collective-permute-done.3 = bf16[256,2048]{1,0:T(8,128)(2,1)} collective-permute-done((bf16[256,2048]{1,0:T(8,128)(2,1)}, bf16[256,2048]{1,0:T(8,128)(2,1)}, u32[]{:S(2)}, u32[]{:S(2)}) %collective-permute-start.3) | collective-permute-done | bytes 1048608 | tf_op jit(solution)/shard_map/ppermute | solution.py:73
  213.7 3.4 fusion.114
  217.2 5.8 multiply_convert_fusion.6
  223.0 3.4 fusion.116
  226.5 3.4 convolution_add_fusion.4
  230.5 5.4 fusion.115
  237.9 18.4 %collective-permute-done.8 = bf16[256,2048]{1,0:T(8,128)(2,1)S(1)} collective-permute-done((bf16[256,2048]{1,0:T(8,128)(2,1)S(1)}, bf16[256,2048]{1,0:T(8,128)(2,1)S(1)}, u32[]{:S(2)}, u32[]{:S(2)}) %collective-permute-start.8) | collective-permute-done | bytes 1048608 | tf_op jit(solution)/shard_map/ppermute | solution.py:68
  258.3 28.3 %collective-permute-done.4 = bf16[256,2048]{1,0:T(8,128)(2,1)S(1)} collective-permute-done((bf16[256,2048]{1,0:T(8,128)(2,1)S(1)}, bf16[256,2048]{1,0:T(8,128)(2,1)S(1)}, u32[]{:S(2)}, u32[]{:S(2)}) %collective-permute-start.4) | collective-permute-done | bytes 1048608 | tf_op jit(solution)/shard_map/ppermute | solution.py:68
  287.0 2.5 collective-permute-start.5
  290.1 34.2 %collective-permute-done.5 = bf16[128,2048]{1,0:T(8,128)(2,1)S(1)} collective-permute-done((bf16[128,2048]{1,0:T(8,128)(2,1)S(1)}, bf16[128,2048]{1,0:T(8,128)(2,1)S(1)}, u32[]{:S(2)}, u32[]{:S(2)}) %collective-permute-start.5) | collective-permute-done | bytes 524320 | tf_op jit(solution)/shard_map/ppermute | solution.py:68
  324.6 22.3 %collective-permute-done.10 = bf16[128,2048]{1,0:T(8,128)(2,1)S(1)} collective-permute-done((bf16[128,2048]{1,0:T(8,128)(2,1)S(1)}, bf16[128,2048]{1,0:T(8,128)(2,1)S(1)}, u32[]{:S(2)}, u32[]{:S(2)}) %collective-permute-start.10) | collective-permute-done | bytes 524320 | tf_op jit(solution)/shard_map/ppermute | solution.py:73
  347.1 9.8 %collective-permute-done.6 = bf16[128,2048]{1,0:T(8,128)(2,1)S(1)} collective-permute-done((bf16[128,2048]{1,0:T(8,128)(2,1)S(1)}, bf16[128,2048]{1,0:T(8,128)(2,1)S(1)}, u32[]{:S(2)}, u32[]{:S(2)}) %collective-permute-start.6) | collective-permute-done | bytes 524320 | tf_op jit(solution)/shard_map/ppermute | solution.py:73
  357.2 22.2 %collective-permute-done.11 = bf16[256,2048]{1,0:T(8,128)(2,1)S(1)} collective-permute-done((bf16[256,2048]{1,0:T(8,128)(2,1)S(1)}, bf16[256,2048]{1,0:T(8,128)(2,1)S(1)}, u32[]{:S(2)}, u32[]{:S(2)}) %collective-permute-start.11) | collective-permute-done | bytes 1048608 | tf_op jit(solution)/shard_map/ppermute | solution.py:73
  379.9 3.9 fusion.19
  383.8 18.0 %collective-permute-done.7 = bf16[256,2048]{1,0:T(8,128)(2,1)S(1)} collective-permute-done((bf16[256,2048]{1,0:T(8,128)(2,1)S(1)}, bf16[256,2048]{1,0:T(8,128)(2,1)S(1)}, u32[]{:S(2)}, u32[]{:S(2)}) %collective-permute-start.7) | collective-permute-done | bytes 1048608 | tf_op jit(solution)/shard_map/ppermute | solution.py:73
  402.3 6.3 convert_add_fusion.1
  410.9 3.6 fusion.25
  414.5 3.6 fusion.28
  418.1 4.6 fusion.13
  422.8 4.8 fusion.12
  427.6 4.6 fusion.57
  432.3 4.6 fusion.47
  436.9 4.6 fusion.45
  441.5 20.8 %multiply_reduce_fusion.2 = (f32[512]{0:T(512)S(1)}, f32[512]{0:T(512)S(1)}, f32[512]{0:T(512)S(1)}, f32[512]{0:T(512)}, f32[512,4096]{1,0:T(8,128)}) fusion(f32[512,4096]{1,0:T(8,128)S(1)} %bitcast.53, f32[512]{0:T(512)S(1)} %copy-done.69, s32[512]{0:T(512)S(1)} %copy-done.63, pred[4096]{0:T(1024)(128)(4,1)S(1)} %bitcast.97, s32[512]{0:T(512)S(1)} %copy-done.59, ...), kind=kOutput, calls=%fused_computation.7 | convolution fusion | flops 578811904 | bytes 68329472 | tf_op jit(solution)/shard_map/dot_general | solution.py:44
  462.3 18.3 %multiply_convert_fusion.2 = (bf16[512,4096]{1,0:T(8,128)(2,1)}, bf16[512,4096]{1,0:T(8,128)(2,1)}, bf16[512,4096]{1,0:T(8,128)(2,1)}) fusion(f32[512,4096]{1,0:T(8,128)} %get-tuple-element.88, f32[512]{0:T(512)S(1)} %get-tuple-element.31, f32[512,4096]{1,0:T(8,128)S(1)} %bitcast.53, f32[512]{0:T(512)S(1)} %copy-done.69, s32[512]{0:T(512)S(1)} %copy-done.63, ...), kind=kLoop, calls=%fused_computation.6 | loop fusion | flops 39845888 | bytes 62951424 | tf_op jit(solution)/shard_map/convert_element_type | solution.py:228
  480.7 3.0 fusion.79
  483.7 8.7 multiply_convert_fusion
  500.8 6.8 convolution_convert_fusion.2
  507.6 5.3 convolution_convert_fusion.1
  512.9 5.2 convolution_convert_fusion
  518.6 4.5 convolution_multiply_fusion
  523.1 3.0 convolution_multiply_fusion.1
  526.1 3.0 convolution_multiply_fusion.2
  529.1 2.9 convolution_multiply_fusion.3
  532.2 17.6 %reduce-scatter.2.cloned.1.call-done = bf16[512,512]{0,1:T(8,128)(2,1)} async-done(((bf16[4096,512]{0,1:T(8,128)(2,1)}), bf16[512,512]{0,1:T(8,128)(2,1)}) %reduce-scatter.2.cloned.1.call-update) | async-done | bytes 524304 | tf_op jit(solution)/shard_map/reduce_scatter | solution.py:238
  558.0 23.2 %collective-permute-done.12 = bf16[256,2048]{1,0:T(8,128)(2,1)S(1)} collective-permute-done((bf16[256,2048]{1,0:T(8,128)(2,1)S(1)}, bf16[256,2048]{1,0:T(8,128)(2,1)S(1)}, u32[]{:S(2)}, u32[]{:S(2)}) %collective-permute-start.12) | collective-permute-done | bytes 1048608 | tf_op jit(solution)/shard_map/ppermute | solution.py:68
  583.7 2.5 collective-permute-start.13
  586.2 2.8 fusion.97
  589.0 2.7 fusion.87
  591.7 185.1 %all-reduce.10.cloned.1.call-done = (bf16[2048,1408]{1,0:T(8,128)(2,1)}, bf16[2048,1408]{1,0:T(8,128)(2,1)}, bf16[1408,2048]{1,0:T(8,128)(2,1)}) async-done(((bf16[2048,1408]{1,0:T(8,128)(2,1)}, bf16[2048,1408]{1,0:T(8,128)(2,1)}, bf16[1408,2048]{1,0:T(8,128)(2,1)}), (bf16[2048,1408]{1,0:T(8,128)(2,1)}, bf16[2048,1408]{1,0:T(8,128)(2,1)}, bf16[1408,2048]{1,0:T(8,128)(2,1)})) %all-reduce.10.cloned.1.call-update) | async-done | bytes 17301520 | tf_op jit(solution)/shard_map/psum | solution.py:272
  776.8 8.6 convert_element_type.279
  785.4 5.2 convert_element_type.281
  790.5 6.2 convert_element_type.283
  804.7 54.0 %all-reduce.6.cloned.1.call-done = bf16[512,2048]{1,0:T(8,128)(2,1)} async-done(((bf16[512,2048]{1,0:T(8,128)(2,1)}), bf16[512,2048]{1,0:T(8,128)(2,1)}) %all-reduce.6.cloned.1.call-update) | async-done | bytes 2097168 | tf_op jit(solution)/shard_map/psum | solution.py:272
  858.7 4.1 convert_element_type.285
  867.1 3.3 collective-permute-done.20
  870.8 17.1 %collective-permute-done.15 = bf16[256,2048]{1,0:T(8,128)(2,1)S(1)} collective-permute-done((bf16[256,2048]{1,0:T(8,128)(2,1)S(1)}, bf16[256,2048]{1,0:T(8,128)(2,1)S(1)}, u32[]{:S(2)}, u32[]{:S(2)}) %collective-permute-start.15) | collective-permute-done | bytes 1048608 | tf_op jit(solution)/shard_map/ppermute | solution.py:73
  890.6 52.6 %all-reduce.8.cloned.1.call-done = (bf16[2048,512]{1,0:T(8,128)(2,1)}, bf16[2048,256]{1,0:T(8,128)(2,1)}, bf16[2048,256]{1,0:T(8,128)(2,1)}) async-done(((bf16[2048,512]{1,0:T(8,128)(2,1)}, bf16[2048,256]{1,0:T(8,128)(2,1)}, bf16[2048,256]{1,0:T(8,128)(2,1)}), (bf16[2048,512]{1,0:T(8,128)(2,1)}, bf16[2048,256]{1,0:T(8,128)(2,1)}, bf16[2048,256]{1,0:T(8,128)(2,1)})) %all-reduce.8.cloned.1.call-update) | async-done | bytes 4194320 | tf_op jit(solution)/shard_map/psum | solution.py:272
  943.2 4.3 convert_element_type.287
  955.5 4.2 fusion.21
  (338 shorter events, 93.0 us)
Async XLA Ops:
  7.2 91.9 %copy-start = (bf16[512,2048]{1,0:T(8,128)(2,1)S(1)}, bf16[512,2048]{1,0:T(8,128)(2,1)}, u32[]{:S(2)}) copy-start(bf16[512,2048]{1,0:T(8,128)(2,1)} %param.20) | copy-start | bytes 6291460
  7.2 51.4 %all-gather.3.cloned.1.call-start = ((), (), s32[]{:S(2)}) async-start(), calls=%async_computation.1 | async-start | bytes 4718592 | tf_op jit(solution)/shard_map/all_gather | solution.py:157
  8.1 21.1 %copy-start.55 = (f32[2048]{0:T(1024)}, f32[2048]{0:T(1024)S(1)}, u32[]{:S(2)}) copy-start(f32[2048]{0:T(1024)S(1)} %convert_element_type.224) | copy-start | bytes 24580
  10.4 18.8 %copy-start.72 = (f32[512]{0:T(512)}, f32[512]{0:T(512)S(1)}, u32[]{:S(2)}) copy-start(f32[512]{0:T(512)S(1)} %fusion.90) | copy-start | bytes 6148
  15.2 63.8 %copy-start.57 = (s32[512]{0:T(512)}, s32[512]{0:T(512)S(1)}, u32[]{:S(2)}) copy-start(s32[512]{0:T(512)S(1)} %get-tuple-element.42) | copy-start | bytes 6148
  16.4 16.6 %copy-start.28 = (f32[512,64]{0,1:T(8,128)}, f32[512,64]{0,1:T(8,128)S(1)}, u32[]{:S(2)}) copy-start(f32[512,64]{0,1:T(8,128)S(1)} %get-tuple-element.77) | copy-start | bytes 393220
  18.4 531.4 %reduce-scatter.2.cloned.1.call-start = ((), (), s32[]{:S(2)}) async-start(), calls=%async_computation.2 | async-start | bytes 4718592 | tf_op jit(solution)/shard_map/reduce_scatter | solution.py:238
  29.2 49.8 %copy-start.61 = (s32[512]{0:T(512)}, s32[512]{0:T(512)S(1)}, u32[]{:S(2)}) copy-start(s32[512]{0:T(512)S(1)} %iota_add_fusion) | copy-start | bytes 6148
  33.2 45.8 %copy-start.30 = (bf16[512,4,128]{0,2,1:T(8,128)(2,1)}, bf16[512,4,128]{0,2,1:T(8,128)(2,1)S(1)}, u32[]{:S(2)}) copy-start(bf16[512,4,128]{0,2,1:T(8,128)(2,1)S(1)} %pad_maximum_fusion.8) | copy-start | bytes 1572868
  72.5 20.5 %copy-start.6 = (f32[512,4096]{1,0:T(8,128)}, f32[512,4096]{1,0:T(8,128)S(1)}, u32[]{:S(2)}) copy-start(f32[512,4096]{1,0:T(8,128)S(1)} %get-tuple-element.83) | copy-start | bytes 25165828
  77.7 17.2 %copy-start.7 = (f32[512,4096]{1,0:T(8,128)}, f32[512,4096]{1,0:T(8,128)S(1)}, u32[]{:S(2)}) copy-start(f32[512,4096]{1,0:T(8,128)S(1)} %get-tuple-element.85) | copy-start | bytes 25165828
  84.6 12.5 %copy-start.8 = (f32[512,4096]{1,0:T(8,128)}, f32[512,4096]{1,0:T(8,128)S(1)}, u32[]{:S(2)}) copy-start(f32[512,4096]{1,0:T(8,128)S(1)} %get-tuple-element.87) | copy-start | bytes 25165828
  85.9 7.1 copy-start.26
  93.0 6.1 copy-start.47
  102.5 25.5 %collective-permute-start = (bf16[256,2048]{1,0:T(8,128)(2,1)S(1)}, bf16[256,2048]{1,0:T(8,128)(2,1)}, u32[]{:S(2)}, u32[]{:S(2)}) collective-permute-start(bf16[256,2048]{1,0:T(8,128)(2,1)S(1)} %dynamic-slice_convert_fusion.3), channel_id=1, source_target_pairs={{0,1},{1,0},{2,3},{3,2},{4,5},{5,4},{6,7},{7,6},{8,9},{9,8},{10,11... | collective-permute-start | bytes 3145736 | tf_op jit(solution)/shard_map/ppermute | solution.py:68
  131.6 54.4 %copy-start.80 = (bf16[2048]{0:T(1024)(128)(2,1)S(1)}, bf16[2048]{0:T(1024)(128)(2,1)}, u32[]{:S(2)}) copy-start(bf16[2048]{0:T(1024)(128)(2,1)} %param.21) | copy-start | bytes 12292
  131.6 25.4 %collective-permute-start.1 = (bf16[128,2048]{1,0:T(8,128)(2,1)S(1)}, bf16[128,2048]{1,0:T(8,128)(2,1)S(1)}, u32[]{:S(2)}, u32[]{:S(2)}) collective-permute-start(bf16[128,2048]{1,0:T(8,128)(2,1)S(1)} %dynamic-slice_convert_fusion.7), channel_id=1, source_target_pairs={{0,2},{1,3},{2,0},{3,1},{4,6},{5,7},{6,4},{7,5},{8,10},{9,11},{10,... | collective-permute-start | bytes 1572872 | tf_op jit(solution)/shard_map/ppermute | solution.py:68
  158.4 25.2 %collective-permute-start.2 = (bf16[128,2048]{1,0:T(8,128)(2,1)S(1)}, bf16[128,2048]{1,0:T(8,128)(2,1)}, u32[]{:S(2)}, u32[]{:S(2)}) collective-permute-start(bf16[128,2048]{1,0:T(8,128)(2,1)S(1)} %add_convert_fusion.4), channel_id=1, source_target_pairs={{0,2},{1,3},{2,0},{3,1},{4,6},{5,7},{6,4},{7,5},{8,10},{9,11},{10,... | collective-permute-start | bytes 1572872 | tf_op jit(solution)/shard_map/ppermute | solution.py:73
  186.0 23.8 %collective-permute-start.3 = (bf16[256,2048]{1,0:T(8,128)(2,1)}, bf16[256,2048]{1,0:T(8,128)(2,1)}, u32[]{:S(2)}, u32[]{:S(2)}) collective-permute-start(bf16[256,2048]{1,0:T(8,128)(2,1)} %pad_maximum_fusion.3), channel_id=1, source_target_pairs={{0,1},{1,0},{2,3},{3,2},{4,5},{5,4},{6,7},{7,6},{8,9},{9,8},{10,11... | collective-permute-start | bytes 3145736 | tf_op jit(solution)/shard_map/ppermute | solution.py:73
  192.5 19.2 %copy-start.3 = (bf16[512,2048]{1,0:T(8,128)(2,1)S(1)}, bf16[512,2048]{1,0:T(8,128)(2,1)}, u32[]{:S(2)}) copy-start(bf16[512,2048]{1,0:T(8,128)(2,1)} %param.13) | copy-start | bytes 6291460
  230.1 26.1 %collective-permute-start.8 = (bf16[256,2048]{1,0:T(8,128)(2,1)S(1)}, bf16[256,2048]{1,0:T(8,128)(2,1)S(1)}, u32[]{:S(2)}, u32[]{:S(2)}) collective-permute-start(bf16[256,2048]{1,0:T(8,128)(2,1)S(1)} %dynamic-slice_convert_fusion.1), channel_id=1, source_target_pairs={{0,1},{1,0},{2,3},{3,2},{4,5},{5,4},{6,7},{7,6},{8,9},{9,8},{10,11... | collective-permute-start | bytes 3145736 | tf_op jit(solution)/shard_map/ppermute | solution.py:68
  236.1 50.5 %collective-permute-start.4 = (bf16[256,2048]{1,0:T(8,128)(2,1)S(1)}, bf16[256,2048]{1,0:T(8,128)(2,1)S(1)}, u32[]{:S(2)}, u32[]{:S(2)}) collective-permute-start(bf16[256,2048]{1,0:T(8,128)(2,1)S(1)} %dynamic-slice_convert_fusion.2), channel_id=1, source_target_pairs={{0,1},{1,0},{2,3},{3,2},{4,5},{5,4},{6,7},{7,6},{8,9},{9,8},{10,11... | collective-permute-start | bytes 3145736 | tf_op jit(solution)/shard_map/ppermute | solution.py:68
  256.6 32.8 %collective-permute-start.9 = (bf16[128,2048]{1,0:T(8,128)(2,1)S(1)}, bf16[128,2048]{1,0:T(8,128)(2,1)S(1)}, u32[]{:S(2)}, u32[]{:S(2)}) collective-permute-start(bf16[128,2048]{1,0:T(8,128)(2,1)S(1)} %dynamic-slice_convert_fusion.5), channel_id=1, source_target_pairs={{0,2},{1,3},{2,0},{3,1},{4,6},{5,7},{6,4},{7,5},{8,10},{9,11},{10,... | collective-permute-start | bytes 1572872 | tf_op jit(solution)/shard_map/ppermute | solution.py:68
  287.0 37.4 %collective-permute-start.5 = (bf16[128,2048]{1,0:T(8,128)(2,1)S(1)}, bf16[128,2048]{1,0:T(8,128)(2,1)S(1)}, u32[]{:S(2)}, u32[]{:S(2)}) collective-permute-start(bf16[128,2048]{1,0:T(8,128)(2,1)S(1)} %dynamic-slice_convert_fusion.6), channel_id=1, source_target_pairs={{0,2},{1,3},{2,0},{3,1},{4,6},{5,7},{6,4},{7,5},{8,10},{9,11},{10,... | collective-permute-start | bytes 1572872 | tf_op jit(solution)/shard_map/ppermute | solution.py:68
  289.6 57.2 %collective-permute-start.10 = (bf16[128,2048]{1,0:T(8,128)(2,1)S(1)}, bf16[128,2048]{1,0:T(8,128)(2,1)S(1)}, u32[]{:S(2)}, u32[]{:S(2)}) collective-permute-start(bf16[128,2048]{1,0:T(8,128)(2,1)S(1)} %add_convert_fusion.2), channel_id=1, source_target_pairs={{0,2},{1,3},{2,0},{3,1},{4,6},{5,7},{6,4},{7,5},{8,10},{9,11},{10,... | collective-permute-start | bytes 1572872 | tf_op jit(solution)/shard_map/ppermute | solution.py:73
  324.5 32.4 %collective-permute-start.6 = (bf16[128,2048]{1,0:T(8,128)(2,1)S(1)}, bf16[128,2048]{1,0:T(8,128)(2,1)S(1)}, u32[]{:S(2)}, u32[]{:S(2)}) collective-permute-start(bf16[128,2048]{1,0:T(8,128)(2,1)S(1)} %add_convert_fusion.3), channel_id=1, source_target_pairs={{0,2},{1,3},{2,0},{3,1},{4,6},{5,7},{6,4},{7,5},{8,10},{9,11},{10,... | collective-permute-start | bytes 1572872 | tf_op jit(solution)/shard_map/ppermute | solution.py:73
  347.0 32.4 %collective-permute-start.11 = (bf16[256,2048]{1,0:T(8,128)(2,1)S(1)}, bf16[256,2048]{1,0:T(8,128)(2,1)S(1)}, u32[]{:S(2)}, u32[]{:S(2)}) collective-permute-start(bf16[256,2048]{1,0:T(8,128)(2,1)S(1)} %pad_maximum_fusion.5), channel_id=1, source_target_pairs={{0,1},{1,0},{2,3},{3,2},{4,5},{5,4},{6,7},{7,6},{8,9},{9,8},{10,11... | collective-permute-start | bytes 3145736 | tf_op jit(solution)/shard_map/ppermute | solution.py:73
  347.1 63.7 %copy-start.66 = (f32[512]{0:T(512)}, f32[512]{0:T(512)S(1)}, u32[]{:S(2)}) copy-start(f32[512]{0:T(512)S(1)} %get-tuple-element.90) | copy-start | bytes 6148
  347.1 71.0 %copy-start.74 = (f32[512]{0:T(512)}, f32[512]{0:T(512)S(1)}, u32[]{:S(2)}) copy-start(f32[512]{0:T(512)S(1)} %get-tuple-element.89) | copy-start | bytes 6148
  347.1 67.4 %copy-start.70 = (f32[512]{0:T(512)}, f32[512]{0:T(512)S(1)}, u32[]{:S(2)}) copy-start(f32[512]{0:T(512)S(1)} %get-tuple-element.92) | copy-start | bytes 6148
  347.1 75.7 %copy-start.68 = (f32[512]{0:T(512)}, f32[512]{0:T(512)S(1)}, u32[]{:S(2)}) copy-start(f32[512]{0:T(512)S(1)} %get-tuple-element.91) | copy-start | bytes 6148
  357.1 44.7 %collective-permute-start.7 = (bf16[256,2048]{1,0:T(8,128)(2,1)S(1)}, bf16[256,2048]{1,0:T(8,128)(2,1)S(1)}, u32[]{:S(2)}, u32[]{:S(2)}) collective-permute-start(bf16[256,2048]{1,0:T(8,128)(2,1)S(1)} %pad_maximum_fusion.4), channel_id=1, source_target_pairs={{0,1},{1,0},{2,3},{3,2},{4,5},{5,4},{6,7},{7,6},{8,9},{9,8},{10,11... | collective-permute-start | bytes 3145736 | tf_op jit(solution)/shard_map/ppermute | solution.py:73
  379.9 22.4 %copy-start.32 = (bf16[512,2048]{1,0:T(8,128)(2,1)S(1)}, bf16[512,2048]{1,0:T(8,128)(2,1)}, u32[]{:S(2)}) copy-start(bf16[512,2048]{1,0:T(8,128)(2,1)} %param.25) | copy-start | bytes 6291460
  401.8 9.0 slice-start
  402.3 8.5 slice-start.1
  410.8 7.3 slice-start.6
  410.8 12.0 %slice-start.2 = ((s8[8388608]{0:T(1024)(128)(4,1)}), s8[4194304]{0:T(1024)(128)(4,1)S(1)}, s32[]{:S(2)}) async-start(s8[8388608]{0:T(1024)(128)(4,1)} %bitcast.52), calls=%async_computation.8 | async-start | bytes 8388608
  414.5 8.3 slice-start.3
  462.3 18.4 %copy-start.31 = (bf16[512,4,128]{0,2,1:T(8,128)(2,1)S(1)}, bf16[512,4,128]{0,2,1:T(8,128)(2,1)}, u32[]{:S(2)}) copy-start(bf16[512,4,128]{0,2,1:T(8,128)(2,1)} %copy-done.30) | copy-start | bytes 1572868
  483.7 8.7 copy-start.15
  499.2 8.3 copy-start.84
  499.2 277.5 %all-reduce.10.cloned.1.call-start = ((), (), s32[]{:S(2)}) async-start(), calls=%async_computation.5 | async-start | bytes 34603008 | tf_op jit(solution)/shard_map/psum | solution.py:272
  500.8 6.8 copy-start.37
  518.1 340.6 %all-reduce.6.cloned.1.call-start = ((), (), s32[]{:S(2)}) async-start(), calls=%async_computation.3 | async-start | bytes 4194304 | tf_op jit(solution)/shard_map/psum | solution.py:272
  556.2 30.0 %copy-start.4 = (bf16[512,2048]{1,0:T(8,128)(2,1)S(1)}, bf16[512,2048]{1,0:T(8,128)(2,1)}, u32[]{:S(2)}) copy-start(bf16[512,2048]{1,0:T(8,128)(2,1)} %param.13) | copy-start | bytes 6291460
  556.2 29.9 %copy-start.56 = (f32[2048]{0:T(1024)S(1)}, f32[2048]{0:T(1024)}, u32[]{:S(2)}) copy-start(f32[2048]{0:T(1024)} %copy-done.55) | copy-start | bytes 24580
  556.2 29.9 %copy-start.73 = (f32[512]{0:T(512)S(1)}, f32[512]{0:T(512)}, u32[]{:S(2)}) copy-start(f32[512]{0:T(512)} %copy-done.72) | copy-start | bytes 6148
  556.4 24.8 %collective-permute-start.12 = (bf16[256,2048]{1,0:T(8,128)(2,1)S(1)}, bf16[256,2048]{1,0:T(8,128)(2,1)S(1)}, u32[]{:S(2)}, u32[]{:S(2)}) collective-permute-start(bf16[256,2048]{1,0:T(8,128)(2,1)S(1)} %dynamic-slice_convert_fusion), channel_id=1, source_target_pairs={{0,1},{1,0},{2,3},{3,2},{4,5},{5,4},{6,7},{7,6},{8,9},{9,8},{10,11... | collective-permute-start | bytes 3145736 | tf_op jit(solution)/shard_map/ppermute | solution.py:68
  583.7 213.1 %collective-permute-start.13 = (bf16[128,2048]{1,0:T(8,128)(2,1)}, bf16[128,2048]{1,0:T(8,128)(2,1)}, u32[]{:S(2)}, u32[]{:S(2)}) collective-permute-start(bf16[128,2048]{1,0:T(8,128)(2,1)} %dynamic-slice_convert_fusion.4), channel_id=1, source_target_pairs={{0,2},{1,3},{2,0},{3,1},{4,6},{5,7},{6,4},{7,5},{8,10},{9,11},{10,... | collective-permute-start | bytes 1572872 | tf_op jit(solution)/shard_map/ppermute | solution.py:68
  776.8 8.6 copy-start.24
  776.8 13.8 %slice-start.8 = ((s8[5767168]{0:T(1024)(128)(4,1)}), s8[4194304]{0:T(1024)(128)(4,1)S(1)}, s32[]{:S(2)}) async-start(s8[5767168]{0:T(1024)(128)(4,1)} %bitcast.58), calls=%async_computation.14 | async-start | bytes 8388608
  796.7 146.4 %all-reduce.8.cloned.1.call-start = ((), (), s32[]{:S(2)}) async-start(), calls=%async_computation.4 | async-start | bytes 8388608 | tf_op jit(solution)/shard_map/psum | solution.py:272
  798.3 64.6 %collective-permute-start.14 = (bf16[128,2048]{1,0:T(8,128)(2,1)S(1)}, bf16[128,2048]{1,0:T(8,128)(2,1)}, u32[]{:S(2)}, u32[]{:S(2)}) collective-permute-start(bf16[128,2048]{1,0:T(8,128)(2,1)S(1)} %add_convert_fusion.1), channel_id=1, source_target_pairs={{0,2},{1,3},{2,0},{3,1},{4,6},{5,7},{6,4},{7,5},{8,10},{9,11},{10,... | collective-permute-start | bytes 1572872 | tf_op jit(solution)/shard_map/ppermute | solution.py:73
  864.1 23.8 %collective-permute-start.15 = (bf16[256,2048]{1,0:T(8,128)(2,1)S(1)}, bf16[256,2048]{1,0:T(8,128)(2,1)S(1)}, u32[]{:S(2)}, u32[]{:S(2)}) collective-permute-start(bf16[256,2048]{1,0:T(8,128)(2,1)S(1)} %pad_maximum_fusion.7), channel_id=1, source_target_pairs={{0,1},{1,0},{2,3},{3,2},{4,5},{5,4},{6,7},{7,6},{8,9},{9,8},{10,11... | collective-permute-start | bytes 3145736 | tf_op jit(solution)/shard_map/ppermute | solution.py:73
  865.6 1.2 collective-permute-start.19
  866.7 3.7 collective-permute-start.20
  870.4 19.6 %collective-permute-start.21 = (f32[2048]{0:T(1024)S(1)}, f32[2048]{0:T(1024)S(1)}, u32[]{:S(2)}, u32[]{:S(2)}) collective-permute-start(f32[2048]{0:T(1024)S(1)} %add.262), channel_id=1, source_target_pairs={{0,16},{4,20},{8,24},{12,28},{16,0},{20,4},{24,8},{28,12},{1,17},{... | collective-permute-start | bytes 24584 | tf_op jit(solution)/shard_map/ppermute | solution.py:87
  889.9 60.6 %collective-permute-start.16 = (f32[2048]{0:T(1024)S(1)}, f32[2048]{0:T(1024)S(1)}, u32[]{:S(2)}, u32[]{:S(2)}) collective-permute-start(f32[2048]{0:T(1024)S(1)} %get-tuple-element.29), channel_id=1, source_target_pairs={{0,4},{4,0},{8,12},{12,8},{16,20},{20,16},{24,28},{28,24},{1,5},{5... | collective-permute-start | bytes 24584 | tf_op jit(solution)/shard_map/ppermute | solution.py:87
  943.2 12.3 %copy-start.21 = (bf16[256,2048]{1,0:T(8,128)(2,1)S(1)}, bf16[256,2048]{1,0:T(8,128)(2,1)}, u32[]{:S(2)}) copy-start(bf16[256,2048]{1,0:T(8,128)(2,1)} %copy-done.20) | copy-start | bytes 3145732
  947.5 8.0 copy-start.5
  947.5 8.0 copy-start.12
  950.5 3.7 collective-permute-start.17
  954.1 6.2 copy-start.1
  954.2 5.6 collective-permute-start.18
  (65 other events, 234.6 us)
Sparse Core Ops, SparseCore 0:
  18.5 40.0 all-gather.2
  499.4 50.4 reduce-scatter.1
  554.6 222.0 all-reduce.9
  796.9 61.8 all-reduce.5
  863.0 80.0 all-reduce.7
